TPU v7x, 32 devices: a whole 2x2x4 slice. The times are simulated.
32 devices in a mesh: front: 2 (over x), column: 4 (over y, core), row: 4 (over z).
Axes of the slice: x: 2, y: 2, z: 4, core: 2. Of those that a mesh axis runs over, the one named last changes fastest.
Arguments:
- cbs: float32 [2, 2, 2048, 2048], P('front', None, 'row', 'column'), may hold values from -4 to 4
- row_map: int32 [2, 2, 16], P('front'), may hold values from 0 to 47, as said below
- col_map: int32 [2, 2, 16], P('front'), may hold values from 0 to 47, as said below
- child_size: int32 [2, 2], P('front'), may hold values from 8 to 16, as said below
- front_diag: float32 [2, 6144], P('front'), may hold values from 0.1 to 200
- panel_order: int32 [2, 4], P('front'), may hold values from 0 to 23, as said below
- pivot_inverse: float32 [2, 4, 256, 256], P('front'), may hold values from -0.2 to 0.8
Outputs:
- factored_front: float32 [2, 6144, 6144], P('front', 'row', 'column')
Inputs may be any that keep to these rules, and one draw needn't show every extreme that they name: `row_map`: entries of one child are distinct. Split the parent tiles into aligned runs of 12 consecutive tiles (tiles t with the same t // 12, the tiles one row owner holds). In each aligned run of 4 entries at most 2 lie in one such aligned parent run, and in every aligned run of 4 entries some aligned parent run gets exactly 2. `col_map`: entries of one child are distinct. Split the parent tiles into aligned runs of 12 consecutive tiles (tiles t with the same t // 12, the tiles one column owner holds). In each aligned run of 4 entries no two lie in the same such aligned parent run. `child_size`: every front has a child of size 16. `panel_order`: distinct within a front. The first and the last panel block are each eliminated by exactly one front.
All inputs are finite; a program needn't handle non-finite values.
Results may differ from a plain program's by a relative error of at most 0.0003.
Values sent between devices are 32-bit elements; how exact they have to be, the bound alone decides.
No kernel may reach another device: no remote copies, remote signals or barrier semaphores. Data moves between devices by JAX's collectives and lax.ppermute only.
A program may use at most 192 MiB of HBM per device.

v0:
```python
import jax
import jax.numpy as jnp
from jax import lax
from jax.sharding import PartitionSpec as P
from jax.experimental import pallas as pl
from jax.experimental.pallas import tpu as pltpu

ORDER = 6144
TILE = 128
PANEL = 256
PANELS = 4
ROWMOST = 2


HIGHEST = lax.Precision.HIGHEST


def broadcast(block, axis, source):
    block = jnp.where(lax.axis_index(axis) == source, block, jnp.zeros_like(block))
    return lax.psum(block, axis)


def exchange_broadcast(block, axis, source):
    size = lax.axis_size(axis)
    if size & (size - 1):
        return broadcast(block, axis, source)
    index = lax.axis_index(axis)
    distance = 1
    while distance < size:
        partner = [(i, i ^ distance) for i in range(size)]
        received = lax.ppermute(block, axis, partner)
        take = (source // distance) % 2 != (index // distance) % 2
        block = jnp.where(take, received, block)
        distance *= 2
    return block


def pack_kernel(sources_ref, blocks_ref, out_ref):
    tile_side = out_ref.shape[-1]
    piece_rows = blocks_ref.shape[2] // tile_side
    piece_cols = blocks_ref.shape[3] // tile_side
    per_child = piece_rows * piece_cols

    def place(slot, carry):
        source = sources_ref[slot]

        @pl.when(source >= 0)
        def _():
            child = source // per_child
            row_start = pl.multiple_of((source // piece_cols) % piece_rows * tile_side, tile_side)
            col_start = pl.multiple_of(source % piece_cols * tile_side, tile_side)
            out_ref[slot] = blocks_ref[
                0, child, pl.ds(row_start, tile_side), pl.ds(col_start, tile_side)
            ]

        @pl.when(source < 0)
        def _():
            out_ref[slot] = jnp.zeros((tile_side, tile_side), out_ref.dtype)

        return carry

    lax.fori_loop(0, out_ref.shape[0], place, 0)


def pack_tiles(blocks, target_dev, dest_count, capacity):
    dest_iota = jnp.arange(dest_count, dtype=jnp.int32)
    matches = (target_dev[:, None] == dest_iota[None, :]).astype(jnp.int32)
    earlier = jnp.cumsum(matches, axis=0) - matches
    position = jnp.sum(earlier * matches, axis=1)
    usable = target_dev < dest_count
    slot_index = jnp.where(usable, target_dev * capacity + position, dest_count * capacity)
    tile_ids = jnp.arange(target_dev.shape[0], dtype=jnp.int32)
    sources = (
        jnp.full((dest_count * capacity,), -1, jnp.int32).at[slot_index].set(tile_ids, mode="drop")
    )
    slots = dest_count * capacity
    payload = pl.pallas_call(
        pack_kernel,
        out_shape=jax.ShapeDtypeStruct((slots, TILE, TILE), blocks.dtype),
        grid_spec=pltpu.PrefetchScalarGridSpec(
            num_scalar_prefetch=1,
            grid=(1,),
            in_specs=[pl.BlockSpec(blocks.shape, lambda i, *_: (0, 0, 0, 0))],
            out_specs=pl.BlockSpec((slots, TILE, TILE), lambda i, *_: (0, 0, 0)),
        ),
    )(sources, blocks)
    return payload.reshape((dest_count, capacity, TILE, TILE))


def assemble_kernel(spots_ref, offset_ref, diag_ref, payload_ref, out_ref):
    rows_total, cols_total = out_ref.shape
    tile_side = payload_ref.shape[-1]
    row_tiles = rows_total // tile_side
    col_tiles = cols_total // tile_side
    offset = offset_ref[0]
    for band in range(row_tiles):
        band_rows = pl.ds(band * tile_side, tile_side)
        row_iota = lax.broadcasted_iota(jnp.int32, (tile_side, cols_total), 0) + band * tile_side
        col_iota = lax.broadcasted_iota(jnp.int32, (tile_side, cols_total), 1)
        out_ref[band_rows, :] = jnp.where(
            row_iota + offset == col_iota, diag_ref[band_rows, :], 0.0
        )

    def add_tile(slot, carry):
        spot = spots_ref[slot]
        tile_row = spot // col_tiles
        tile_col = spot % col_tiles

        @pl.when(tile_row < row_tiles)
        def _():
            row_start = pl.multiple_of(tile_row * tile_side, tile_side)
            col_start = pl.multiple_of(tile_col * tile_side, tile_side)
            window = (pl.ds(row_start, tile_side), pl.ds(col_start, tile_side))
            out_ref[window] = out_ref[window] + payload_ref[slot]

        return carry

    lax.fori_loop(0, payload_ref.shape[0], add_tile, 0)


def scatter_tiles(payload, labels, diag_part, offset, local_rows, local_cols):
    tile_side = payload.shape[-1]
    tiles = payload.reshape(-1, tile_side, tile_side)
    slots = tiles.shape[0]
    return pl.pallas_call(
        assemble_kernel,
        out_shape=jax.ShapeDtypeStruct((local_rows, local_cols), jnp.float32),
        grid_spec=pltpu.PrefetchScalarGridSpec(
            num_scalar_prefetch=2,
            grid=(1,),
            in_specs=[
                pl.BlockSpec((local_rows, 1), lambda i, *_: (0, 0)),
                pl.BlockSpec((slots, tile_side, tile_side), lambda i, *_: (0, 0, 0)),
            ],
            out_specs=pl.BlockSpec((local_rows, local_cols), lambda i, *_: (0, 0)),
        ),
    )(labels.reshape(-1), offset.reshape(1), diag_part.reshape(local_rows, 1), tiles)


def arrival_labels(
    row_map, col_map, child_size, groups, row_devs, col_devs, piece_rows, piece_cols,
    row_tiles, col_tiles, sentinel,
):
    children, side = row_map.shape[1], row_map.shape[2]
    span = children * side
    maps = jnp.concatenate(
        [row_map[0].reshape(-1), col_map[0].reshape(-1), child_size[0].reshape(-1)]
    )
    every = lax.all_gather(maps, "front")
    front_id = lax.axis_index("front")
    row_maps = every[:, :span].reshape(groups, children, side)[:, front_id]
    col_maps = every[:, span : 2 * span].reshape(groups, children, side)[:, front_id]
    sizes = every[:, 2 * span :].reshape(groups, children)[:, front_id]
    child_rows = (
        jnp.arange(row_devs, dtype=jnp.int32)[:, None] * piece_rows
        + jnp.arange(piece_rows, dtype=jnp.int32)[None, :]
    )
    child_cols = (
        jnp.arange(col_devs, dtype=jnp.int32)[:, None] * piece_cols
        + jnp.arange(piece_cols, dtype=jnp.int32)[None, :]
    )
    parent_rows = row_maps[:, child_rows]
    parent_cols = col_maps[:, child_cols]
    hit_rows = (child_rows[None] < sizes[:, None, None]) & (
        parent_rows // row_tiles == lax.axis_index("row")
    )
    hit_cols = (child_cols[None] < sizes[:, None, None]) & (
        parent_cols // col_tiles == lax.axis_index("column")
    )
    hit = hit_cols[:, :, None, None, :] & hit_rows[:, None, :, :, None]
    spot = (parent_rows % row_tiles)[:, None, :, :, None] * col_tiles + (
        parent_cols % col_tiles
    )[:, :, None, None, :]
    sources = groups * col_devs * row_devs
    hit = hit.reshape(sources, piece_rows * piece_cols).astype(jnp.int32)
    spot = jnp.broadcast_to(
        spot, (groups, col_devs, row_devs, piece_rows, piece_cols)
    ).reshape(sources, piece_rows * piece_cols)
    rank = jnp.cumsum(hit, axis=1) - hit
    slots = []
    for slot in range(ROWMOST):
        chosen = (hit == 1) & (rank == slot)
        slots.append(
            jnp.where(
                jnp.any(chosen, axis=1), jnp.sum(jnp.where(chosen, spot, 0), axis=1), sentinel
            )
        )
    return jnp.stack(slots, axis=1)


def body(cbs, row_map, col_map, child_size, front_diag, panel_order, pivot_inverse):
    groups = lax.axis_size("front")
    row_devs = lax.axis_size("row")
    col_devs = lax.axis_size("column")
    row_id = lax.axis_index("row")
    col_id = lax.axis_index("column")
    children = cbs.shape[1]
    piece_rows = cbs.shape[2] // TILE
    piece_cols = cbs.shape[3] // TILE
    local_rows = ORDER // row_devs
    local_cols = ORDER // col_devs
    row_tiles = local_rows // TILE
    col_tiles = local_cols // TILE
    sentinel = row_tiles * col_tiles
    child_rows = row_id * piece_rows + jnp.arange(piece_rows, dtype=jnp.int32)
    child_cols = col_id * piece_cols + jnp.arange(piece_cols, dtype=jnp.int32)
    parent_rows = lax.dynamic_slice_in_dim(row_map[0], row_id * piece_rows, piece_rows, 1)
    parent_cols = lax.dynamic_slice_in_dim(col_map[0], col_id * piece_cols, piece_cols, 1)
    live_rows = child_rows[None, :] < child_size[0][:, None]
    live_cols = child_cols[None, :] < child_size[0][:, None]
    owner_rows = parent_rows // row_tiles
    owner_cols = parent_cols // col_tiles
    target_spot = (
        (parent_rows - owner_rows * row_tiles)[:, :, None] * col_tiles
        + (parent_cols - owner_cols * col_tiles)[:, None, :]
    ).reshape(-1)
    usable = (live_rows[:, :, None] & live_cols[:, None, :]).reshape(-1)
    inner_dest = (owner_cols[:, None, :] * row_devs + owner_rows[:, :, None]).reshape(-1)
    all_devices = groups * row_devs * col_devs
    front_ids = jnp.arange(children, dtype=jnp.int32)[:, None]
    whole_dest = (front_ids * (row_devs * col_devs) + inner_dest.reshape(children, -1)).reshape(-1)
    whole_target = jnp.where(usable, whole_dest, all_devices)
    payload = pack_tiles(cbs, whole_target, all_devices, ROWMOST)
    arrived = lax.all_to_all(
        payload, ("front", "column", "row"), split_axis=0, concat_axis=0, tiled=True
    )
    arrived_labels = arrival_labels(
        row_map, col_map, child_size, groups, row_devs, col_devs, piece_rows, piece_cols,
        row_tiles, col_tiles, sentinel,
    )
    row_glob = row_id * local_rows + jnp.arange(local_rows, dtype=jnp.int32)
    col_glob = col_id * local_cols + jnp.arange(local_cols, dtype=jnp.int32)
    diag_part = lax.dynamic_slice_in_dim(front_diag[0], row_id * local_rows, local_rows)
    diag_offset = (row_id * local_rows - col_id * local_cols).astype(jnp.int32)
    matrix = scatter_tiles(arrived, arrived_labels, diag_part, diag_offset, local_rows, local_cols)
    order_row = panel_order[0]
    inverses = pivot_inverse[0]
    panel_rows = local_rows // PANEL
    panel_cols = local_cols // PANEL
    row_block = row_glob // PANEL
    col_block = col_glob // PANEL

    def strip_bounds(step_index):
        pivot_block = order_row[step_index]
        return (
            pivot_block // panel_cols,
            pivot_block // panel_rows,
            pivot_block % panel_cols * PANEL,
            pivot_block % panel_rows * PANEL,
        )

    def actives(step_index):
        chosen = order_row[: step_index + 1]
        active_rows = jnp.all(row_block[:, None] != chosen[None, :], axis=1)
        active_cols = jnp.all(col_block[:, None] != chosen[None, :], axis=1)
        return (active_rows, active_cols)

    def current_strips(matrix, step_index):
        col_owner, row_owner, col_offset, row_offset = strip_bounds(step_index)
        return (
            lax.dynamic_slice_in_dim(matrix, col_offset, PANEL, 1),
            lax.dynamic_slice_in_dim(matrix, row_offset, PANEL, 0),
        )

    def share_strips(col_strip, row_strip, step_index):
        col_owner, row_owner, col_offset, row_offset = strip_bounds(step_index)
        owner_left = jnp.dot(
            col_strip, inverses[step_index], precision=HIGHEST, preferred_element_type=jnp.float32
        )
        left_strip = exchange_broadcast(owner_left, "column", col_owner)
        top_strip = lax.psum(row_strip, "row")
        return (left_strip, top_strip)

    def owned_rows(row_strip, step_index):
        col_owner, row_owner, col_offset, row_offset = strip_bounds(step_index)
        return jnp.where(row_id == row_owner, row_strip, jnp.zeros_like(row_strip))

    first_col, first_row = current_strips(matrix, 0)
    left_strip, top_strip = share_strips(first_col, owned_rows(first_row, 0), 0)
    for step_index in range(PANELS):
        if step_index + 1 < PANELS:
            active_rows, active_cols = actives(step_index)
            next_col, next_row = current_strips(matrix, step_index + 1)
            col_owner, row_owner, col_offset, row_offset = strip_bounds(step_index + 1)
            top_part = lax.dynamic_slice_in_dim(top_strip, col_offset, PANEL, 1)
            left_part = lax.dynamic_slice_in_dim(left_strip, row_offset, PANEL, 0)
            next_row = jnp.where(
                active_cols[None, :],
                next_row
                - jnp.dot(
                    left_part, top_strip, precision=HIGHEST, preferred_element_type=jnp.float32
                ),
                next_row,
            )
            next_row = owned_rows(next_row, step_index + 1)
            next_row, next_col = lax.optimization_barrier((next_row, next_col))
            next_col = jnp.where(
                active_rows[:, None],
                next_col
                - jnp.dot(
                    left_strip, top_part, precision=HIGHEST, preferred_element_type=jnp.float32
                ),
                next_col,
            )
            left_next, top_next = share_strips(next_col, next_row, step_index + 1)
        eliminate_matrix = matrix
        eliminate_active_rows, eliminate_active_cols = actives(step_index)
        product = jnp.dot(
            left_strip, top_strip, precision=HIGHEST, preferred_element_type=jnp.float32
        )
        eliminate_matrix = jnp.where(
            eliminate_active_rows[:, None] & eliminate_active_cols[None, :],
            eliminate_matrix - product,
            eliminate_matrix,
        )
        eliminate_col_owner, eliminate_row_owner, eliminate_col_offset, eliminate_row_offset = (
            strip_bounds(step_index)
        )
        present = lax.dynamic_slice_in_dim(eliminate_matrix, eliminate_col_offset, PANEL, 1)
        fresh_col = jnp.where(
            (col_id == eliminate_col_owner) & eliminate_active_rows[:, None], left_strip, present
        )
        matrix = lax.dynamic_update_slice_in_dim(
            eliminate_matrix, fresh_col, eliminate_col_offset, 1
        )
        if step_index + 1 < PANELS:
            left_strip, top_strip = (left_next, top_next)
    return matrix[None]


def solution(mesh):
    placed = (
        P("front", None, "row", "column"),
        P("front", None, None),
        P("front", None, None),
        P("front", None),
        P("front", None),
        P("front", None),
        P("front", None, None, None),
    )
    return jax.shard_map(
        body, mesh=mesh, in_specs=placed, out_specs=P("front", "row", "column"), check_vma=False
    )
```

profile of v0, /device:TPU:0, one launch (start us, length us, event | category | flops | bytes accessed | tf_op | source)
XLA Modules:
  0.0 472.9 jit_solution(1619641422996455370)
XLA Ops:
  9.2 1.2 scatter_custom_fusion.sources_ref
  10.4 6.2 %shard_map.73 = f32[64,128,128]{2,1,0:T(8,128)} custom-call(s32[64]{0:T(128)} %scatter_custom_fusion.sources_ref, f32[1,2,512,512]{3,2,1,0:T(8,128)} %blocks_ref.1), custom_call_target="tpu_custom_call" | custom-call | tf_op jit(solution)/shard_map/pallas_call | solution.py:77
  16.6 7.4 %all-to-all-start = ((f32[32,2,128,128]{3,2,1,0:T(8,128)}), f32[32,2,128,128]{3,2,1,0:T(8,128)}, u32[]{:S(2)}, u32[]{:S(2)}) async-start(f32[32,2,128,128]{3,2,1,0:T(8,128)} %bitcast.143), calls=%async_computation | async-start | bytes 8388608 | tf_op jit(solution)/shard_map/all_to_all | solution.py:224
  27.0 17.4 %all-reduce = s32[132]{0:T(256)S(1)} all-reduce(s32[132]{0:T(256)S(1)} %add_dynamic-update-slice_fusion), channel_id=2, replica_groups=mesh['front'=2,'column'=4,'row'=4] {'front'}, use_global_device_ids=true, to_apply=%add | all-reduce | flops 132 | bytes 1056
  50.8 63.8 %all-to-all-done = f32[32,2,128,128]{3,2,1,0:T(8,128)} async-done(((f32[32,2,128,128]{3,2,1,0:T(8,128)}), f32[32,2,128,128]{3,2,1,0:T(8,128)}, u32[]{:S(2)}, u32[]{:S(2)}) %all-to-all-start) | async-done | bytes 4194336 | tf_op jit(solution)/shard_map/all_to_all | solution.py:224
  114.5 9.9 %shard_map.74 = f32[1536,1536]{1,0:T(8,128)} custom-call(s32[64]{0:T(128)} %reshape.602.spots_ref, s32[1]{0:T(128)} %bitcast.16.offset_ref, f32[1536,1]{1,0:T(8,128)} %copy.73.diag_ref, f32[64,128,128]{2,1,0:T(8,128)} %bitcast.25.payload_ref), custom_call_target="tpu_custom_call" | custom-call | tf_op jit(solution)/shard_map/pallas_call | solution.py:125
  124.4 2.9 fusion.9
  127.3 1.7 collective-permute-start
  130.3 1.9 collective-permute-done
  132.2 1.7 broadcast_select_fusion.6
  133.9 1.5 collective-permute-start.1
  135.4 2.6 dynamic-slice_select_fusion
  140.7 2.7 constant_dynamic-slice_fusion.2
  143.4 25.9 %collective-permute-done.1 = f32[1536,256]{1,0:T(8,128)} collective-permute-done((f32[1536,256]{1,0:T(8,128)S(1)}, f32[1536,256]{1,0:T(8,128)}, u32[]{:S(2)}, u32[]{:S(2)}) %collective-permute-start.1) | collective-permute-done | bytes 1572896 | tf_op jit(solution)/shard_map/ppermute | solution.py:31
  169.3 1.7 broadcast_select_fusion.7
  171.1 35.9 %all-reduce.6.cloned.1.call-done = f32[256,1536]{1,0:T(8,128)} async-done(((f32[256,1536]{1,0:T(8,128)}), f32[256,1536]{1,0:T(8,128)}) %all-reduce.6.cloned.1.call-update) | async-done | bytes 1572880 | tf_op jit(solution)/shard_map/psum | solution.py:271
  207.0 4.7 fusion.8
  211.7 2.9 fusion.6
  214.5 3.5 fusion.15
  221.8 1.6 broadcast_select_fusion.4
  223.4 1.5 collective-permute-start.3
  224.9 11.7 %subtract_select_fusion.3 = f32[1536,1536]{1,0:T(8,128)S(1)} fusion(f32[1536,1536]{1,0:T(8,128)} %shard_map.74, f32[1536,256]{1,0:T(8,128)S(1)} %broadcast_select_fusion.7, f32[256,1536]{1,0:T(8,128)S(1)} %copy-done.4, pred[1536]{0:T(1024)(128)(4,1)S(1)} %get-tuple-element.46, pred[1536]{0:T(1024)(128)(4,1)S(1)} %get-tuple-element.47), kind=kOutput, calls=%fused_computation.6 | convolution fusion | flops 7254835200 | bytes 22023168 | tf_op jit(solution)/shard_map/dot_general | solution.py:308
  237.2 3.7 copy-done.2
  240.9 1.3 constant_dynamic-slice_fusion.1
  242.2 17.7 %collective-permute-done.3 = f32[1536,256]{1,0:T(8,128)S(1)} collective-permute-done((f32[1536,256]{1,0:T(8,128)S(1)}, f32[1536,256]{1,0:T(8,128)S(1)}, u32[]{:S(2)}, u32[]{:S(2)}) %collective-permute-start.3) | collective-permute-done | bytes 1572896 | tf_op jit(solution)/shard_map/ppermute | solution.py:31
  260.1 29.2 %all-reduce.8.cloned.1.call-done = f32[256,1536]{1,0:T(8,128)} async-done(((f32[256,1536]{1,0:T(8,128)}), f32[256,1536]{1,0:T(8,128)}) %all-reduce.8.cloned.1.call-update) | async-done | bytes 1572880 | tf_op jit(solution)/shard_map/psum | solution.py:271
  289.3 4.7 fusion.5
  294.0 2.9 fusion.3
  296.9 3.5 fusion.13
  302.6 1.5 collective-permute-done.4
  304.1 1.6 broadcast_select_fusion.2
  305.7 1.5 collective-permute-start.5
  307.3 11.6 %subtract_select_fusion.2 = f32[1536,1536]{1,0:T(8,128)S(1)} fusion(f32[1536,1536]{1,0:T(8,128)} %copy-done.2, f32[1536,256]{1,0:T(8,128)S(1)} %broadcast_select_fusion.5, f32[256,1536]{1,0:T(8,128)S(1)} %copy-done.5, pred[1536]{0:T(1024)(128)(4,1)S(1)} %get-tuple-element.24, pred[1536]{0:T(1024)(128)(4,1)S(1)} %get-tuple-element.23), kind=kOutput, calls=%fused_computation.5 | convolution fusion | flops 7254835200 | bytes 22023168 | tf_op jit(solution)/shard_map/dot_general | solution.py:308
  319.4 3.7 copy-done.3
  323.3 19.0 %collective-permute-done.5 = f32[1536,256]{1,0:T(8,128)S(1)} collective-permute-done((f32[1536,256]{1,0:T(8,128)S(1)}, f32[1536,256]{1,0:T(8,128)S(1)}, u32[]{:S(2)}, u32[]{:S(2)}) %collective-permute-start.5) | collective-permute-done | bytes 1572896 | tf_op jit(solution)/shard_map/ppermute | solution.py:31
  342.4 28.3 %all-reduce.10.cloned.1.call-done = f32[256,1536]{1,0:T(8,128)} async-done(((f32[256,1536]{1,0:T(8,128)}), f32[256,1536]{1,0:T(8,128)}) %all-reduce.10.cloned.1.call-update) | async-done | bytes 1572880 | tf_op jit(solution)/shard_map/psum | solution.py:271
  370.8 4.6 fusion.2
  375.4 2.4 fusion
  377.8 2.4 fusion.11
  381.3 2.5 collective-permute-done.6
  383.8 1.7 broadcast_select_fusion
  385.5 1.4 collective-permute-start.7
  387.1 13.4 %subtract_select_fusion.1 = f32[1536,1536]{1,0:T(8,128)} fusion(f32[1536,1536]{1,0:T(8,128)} %copy-done.3, f32[1536,256]{1,0:T(8,128)S(1)} %broadcast_select_fusion.3, f32[256,1536]{1,0:T(8,128)} %all-reduce.10.cloned.1.call-done, pred[1536]{0:T(1024)(128)(4,1)S(1)} %get-tuple-element.22, pred[1536]{0:T(1024)(128)(4,1)S(1)} %get-tuple-element.21), kind=kOutput, calls=%fused_computation.4 | convolution fusion | flops 7254835200 | bytes 22023168 | tf_op jit(solution)/shard_map/dot_general | solution.py:308
  400.5 2.9 select_dynamic-update-slice_fusion
  403.5 45.3 %all-reduce.12.cloned.1.call-done = f32[256,1536]{1,0:T(8,128)} async-done(((f32[256,1536]{1,0:T(8,128)}), f32[256,1536]{1,0:T(8,128)}) %all-reduce.12.cloned.1.call-update) | async-done | bytes 1572880 | tf_op jit(solution)/shard_map/psum | solution.py:271
  448.8 11.8 %subtract_select_fusion = f32[1536,1536]{1,0:T(8,128)S(1)} fusion(f32[1536,1536]{1,0:T(8,128)} %select_dynamic-update-slice_fusion, f32[256,1536]{1,0:T(8,128)} %all-reduce.12.cloned.1.call-done, pred[1536]{0:T(1024)(128)(4,1)S(1)} %get-tuple-element.20, pred[1536]{0:T(1024)(128)(4,1)S(1)} %get-tuple-element.19, f32[1536,256]{1,0:T(8,128)} %collective-permute-done.7, ...), kind=kOutput, calls=%fused_computation.3 | convolution fusion | flops 7255228416 | bytes 23596032 | tf_op jit(solution)/shard_map/dot_general | solution.py:308
  460.6 3.7 copy.82
  464.3 1.5 bitcast_dynamic-update-slice_fusion
  (128 shorter events, 16.2 us)
Async XLA Ops:
  6.5 43.0 %copy-start = (f32[1,6144]{1,0:T(1,128)S(1)}, f32[1,6144]{1,0:T(1,128)}, u32[]{:S(2)}) copy-start(f32[1,6144]{1,0:T(1,128)} %param.11) | copy-start | bytes 73732
  16.6 7.5 %copy-start.9 = (s32[1,2,16]{2,1,0:T(2,128)S(1)}, s32[1,2,16]{2,1,0:T(2,128)}, u32[]{:S(2)}) copy-start(s32[1,2,16]{2,1,0:T(2,128)} %param.8) | copy-start | bytes 388
  16.6 7.6 %copy-start.10 = (s32[1,2,16]{2,1,0:T(2,128)S(1)}, s32[1,2,16]{2,1,0:T(2,128)}, u32[]{:S(2)}) copy-start(s32[1,2,16]{2,1,0:T(2,128)} %param.9) | copy-start | bytes 388
  16.6 7.7 %copy-start.7 = (s32[1,4]{1,0:T(1,128)S(1)}, s32[1,4]{1,0:T(1,128)}, u32[]{:S(2)}) copy-start(s32[1,4]{1,0:T(1,128)} %param.12) | copy-start | bytes 52
  16.6 9.0 %copy-start.11 = (u32[32]{0:T(128)S(1)}, u32[32]{0:T(128)}, u32[]{:S(2)}) copy-start(u32[32]{0:T(128)} %constant.349) | copy-start | bytes 388
  16.6 10.2 %copy-start.8 = (s32[1,2]{1,0:T(1,128)S(1)}, s32[1,2]{1,0:T(1,128)}, u32[]{:S(2)}) copy-start(s32[1,2]{1,0:T(1,128)} %param.10) | copy-start | bytes 28
  16.6 97.9 %all-to-all-start = ((f32[32,2,128,128]{3,2,1,0:T(8,128)}), f32[32,2,128,128]{3,2,1,0:T(8,128)}, u32[]{:S(2)}, u32[]{:S(2)}) async-start(f32[32,2,128,128]{3,2,1,0:T(8,128)} %bitcast.143), calls=%async_computation | async-start | bytes 8388608 | tf_op jit(solution)/shard_map/all_to_all | solution.py:224
  24.0 182.9 %all-reduce.6.cloned.1.call-start = ((), (), s32[]{:S(2)}) async-start(), calls=%async_computation.1 | async-start | bytes 3145728 | tf_op jit(solution)/shard_map/psum | solution.py:271
  127.3 4.9 %collective-permute-start = (f32[1536,256]{1,0:T(8,128)S(1)}, f32[1536,256]{1,0:T(8,128)}, u32[]{:S(2)}, u32[]{:S(2)}) collective-permute-start(f32[1536,256]{1,0:T(8,128)S(1)} %fusion.9), channel_id=1, source_target_pairs={{0,4},{4,0},{8,12},{12,8},{1,5},{5,1},{9,13},{13,9},{2,6},{6,2},{1... | collective-permute-start | bytes 4718600 | tf_op jit(solution)/shard_map/ppermute | solution.py:31
  133.9 35.4 %collective-permute-start.1 = (f32[1536,256]{1,0:T(8,128)S(1)}, f32[1536,256]{1,0:T(8,128)}, u32[]{:S(2)}, u32[]{:S(2)}) collective-permute-start(f32[1536,256]{1,0:T(8,128)S(1)} %broadcast_select_fusion.6), channel_id=1, source_target_pairs={{0,8},{4,12},{8,0},{12,4},{1,9},{5,13},{9,1},{13,5},{2,10},{6,14},... | collective-permute-start | bytes 4718600 | tf_op jit(solution)/shard_map/ppermute | solution.py:31
  138.1 151.2 %all-reduce.8.cloned.1.call-start = ((), (), s32[]{:S(2)}) async-start(), calls=%async_computation.2 | async-start | bytes 3145728 | tf_op jit(solution)/shard_map/psum | solution.py:271
  207.0 4.7 copy-start.4
  218.0 3.8 collective-permute-start.2
  220.8 149.9 %all-reduce.10.cloned.1.call-start = ((), (), s32[]{:S(2)}) async-start(), calls=%async_computation.3 | async-start | bytes 3145728 | tf_op jit(solution)/shard_map/psum | solution.py:271
  223.4 36.5 %collective-permute-start.3 = (f32[1536,256]{1,0:T(8,128)S(1)}, f32[1536,256]{1,0:T(8,128)S(1)}, u32[]{:S(2)}, u32[]{:S(2)}) collective-permute-start(f32[1536,256]{1,0:T(8,128)S(1)} %broadcast_select_fusion.4), channel_id=1, source_target_pairs={{0,8},{4,12},{8,0},{12,4},{1,9},{5,13},{9,1},{13,5},{2,10},{6,14},... | collective-permute-start | bytes 4718600 | tf_op jit(solution)/shard_map/ppermute | solution.py:31
  237.2 3.7 copy-start.2
  289.3 4.7 copy-start.5
  300.4 3.8 collective-permute-start.4
  302.3 146.4 %all-reduce.12.cloned.1.call-start = ((), (), s32[]{:S(2)}) async-start(), calls=%async_computation.4 | async-start | bytes 3145728 | tf_op jit(solution)/shard_map/psum | solution.py:271
  305.7 36.5 %collective-permute-start.5 = (f32[1536,256]{1,0:T(8,128)S(1)}, f32[1536,256]{1,0:T(8,128)S(1)}, u32[]{:S(2)}, u32[]{:S(2)}) collective-permute-start(f32[1536,256]{1,0:T(8,128)S(1)} %broadcast_select_fusion.2), channel_id=1, source_target_pairs={{0,8},{4,12},{8,0},{12,4},{1,9},{5,13},{9,1},{13,5},{2,10},{6,14},... | collective-permute-start | bytes 4718600 | tf_op jit(solution)/shard_map/ppermute | solution.py:31
  319.3 3.7 copy-start.3
  380.2 1.1 copy-start.6
  380.2 3.6 collective-permute-start.6
  385.5 63.2 %collective-permute-start.7 = (f32[1536,256]{1,0:T(8,128)S(1)}, f32[1536,256]{1,0:T(8,128)}, u32[]{:S(2)}, u32[]{:S(2)}) collective-permute-start(f32[1536,256]{1,0:T(8,128)S(1)} %broadcast_select_fusion), channel_id=1, source_target_pairs={{0,8},{4,12},{8,0},{12,4},{1,9},{5,13},{9,1},{13,5},{2,10},{6,14},... | collective-permute-start | bytes 4718600 | tf_op jit(solution)/shard_map/ppermute | solution.py:31
  464.3 1.5 copy-start.1
Sparse Core Ops, SparseCore 0:
  138.2 68.7 all-reduce.5
  221.0 68.3 all-reduce.7
  302.4 68.3 all-reduce.9
  380.4 68.2 all-reduce.11
where the time goes:
time: 482 us; the launch traced here: 473 us
  waiting for transfers between devices  272 us (56%)
  matrix products  82.8 us (17%)
  local copies, waits for them, and re-layouts  25 us (5%)
  between operations  22.4 us (5%)
  other arithmetic  21.7 us (5%)
  blocking collectives  17.4 us (4%)
  Pallas kernels  16 us (3%)
  starting transfers between devices  15.8 us (3%)
    psum x4, waiting for transfers between devices, share_strips(): top_strip = lax.psum(row_strip, 'row')  139 us
    ppermute x8, waiting for transfers between devices, exchange_broadcast(): received = lax.ppermute(block, axis, partner)  69.1 us
    all_to_all x1, waiting for transfers between devices, body(): lax.all_to_all(payload, ('front', 'column', 'row'), split_axis=0, concat_...  63.8 us
    dot_general x4, matrix products, body(): jnp.dot(left_strip, top_strip, precision=HIGHEST, preferred_element_type=...  48.6 us
    unnamed x1, blocking collectives  17.4 us
    dot_general x3, matrix products, body(): jnp.dot(left_part, top_strip, precision=HIGHEST, preferred_element_type=j...  14 us
    unnamed x27, local copies, waits for them, and re-layouts  12.8 us
    dot_general x4, matrix products, share_strips(): jnp.dot(col_strip, inverses[step_index], precision=HIGHEST, preferred_ele...  12.2 us
  transfers between devices with their start and end apart: 13, of which 12 were waited for; matrix products, arithmetic and copies ran while one was open for 14% of the time, Pallas kernels for 0%

commit v1 on v0

--- a/solution.py
+++ b/solution.py
@@ -88,29 +88,21 @@
 
 
 def assemble_kernel(spots_ref, offset_ref, diag_ref, payload_ref, out_ref):
-    rows_total, cols_total = out_ref.shape
+    band_rows, cols_total = out_ref.shape
     tile_side = payload_ref.shape[-1]
-    row_tiles = rows_total // tile_side
     col_tiles = cols_total // tile_side
-    offset = offset_ref[0]
-    for band in range(row_tiles):
-        band_rows = pl.ds(band * tile_side, tile_side)
-        row_iota = lax.broadcasted_iota(jnp.int32, (tile_side, cols_total), 0) + band * tile_side
-        col_iota = lax.broadcasted_iota(jnp.int32, (tile_side, cols_total), 1)
-        out_ref[band_rows, :] = jnp.where(
-            row_iota + offset == col_iota, diag_ref[band_rows, :], 0.0
-        )
+    band = pl.program_id(0)
+    row_iota = lax.broadcasted_iota(jnp.int32, (band_rows, cols_total), 0) + band * band_rows
+    col_iota = lax.broadcasted_iota(jnp.int32, (band_rows, cols_total), 1)
+    out_ref[...] = jnp.where(row_iota + offset_ref[0] == col_iota, diag_ref[...], 0.0)
 
     def add_tile(slot, carry):
         spot = spots_ref[slot]
-        tile_row = spot // col_tiles
-        tile_col = spot % col_tiles
-
-        @pl.when(tile_row < row_tiles)
+
+        @pl.when(spot // col_tiles == band)
         def _():
-            row_start = pl.multiple_of(tile_row * tile_side, tile_side)
-            col_start = pl.multiple_of(tile_col * tile_side, tile_side)
-            window = (pl.ds(row_start, tile_side), pl.ds(col_start, tile_side))
+            col_start = pl.multiple_of(spot % col_tiles * tile_side, tile_side)
+            window = (slice(None), pl.ds(col_start, tile_side))
             out_ref[window] = out_ref[window] + payload_ref[slot]
 
         return carry
@@ -127,12 +119,12 @@
         out_shape=jax.ShapeDtypeStruct((local_rows, local_cols), jnp.float32),
         grid_spec=pltpu.PrefetchScalarGridSpec(
             num_scalar_prefetch=2,
-            grid=(1,),
+            grid=(local_rows // tile_side,),
             in_specs=[
-                pl.BlockSpec((local_rows, 1), lambda i, *_: (0, 0)),
+                pl.BlockSpec((tile_side, 1), lambda i, *_: (i, 0)),
                 pl.BlockSpec((slots, tile_side, tile_side), lambda i, *_: (0, 0, 0)),
             ],
-            out_specs=pl.BlockSpec((local_rows, local_cols), lambda i, *_: (0, 0)),
+            out_specs=pl.BlockSpec((tile_side, local_cols), lambda i, *_: (i, 0)),
         ),
     )(labels.reshape(-1), offset.reshape(1), diag_part.reshape(local_rows, 1), tiles)
 
@@ -276,7 +268,9 @@
         return jnp.where(row_id == row_owner, row_strip, jnp.zeros_like(row_strip))
 
     first_col, first_row = current_strips(matrix, 0)
-    left_strip, top_strip = share_strips(first_col, owned_rows(first_row, 0), 0)
+    first_row = owned_rows(first_row, 0)
+    first_row, first_col = lax.optimization_barrier((first_row, first_col))
+    left_strip, top_strip = share_strips(first_col, first_row, 0)
     for step_index in range(PANELS):
         if step_index + 1 < PANELS:
             active_rows, active_cols = actives(step_index)

time: 482 us -> 500 us (1.037)
  Pallas kernels: 16 us -> 31.1 us
  waiting for transfers between devices: 272 us -> 277 us
    pallas_call x1, Pallas kernels: 9.88 us -> 24.9 us  [scatter_tiles(): pl.pallas_call(assemble_kernel, out_shape=jax.ShapeDtypeStruct((local_row...]
    ppermute x8, waiting for transfers between devices: 69.1 us -> 77.6 us  [exchange_broadcast(): received = lax.ppermute(block, axis, partner)]
  transfers between devices with their start and end apart: 13 -> 13, of which waited for: 12 -> 12; matrix products, arithmetic and copies ran while one was open for 14% -> 12% of each run, Pallas kernels for 0% -> 0%
where the time goes in v1:
time: 500 us; the launch traced here: 492 us
  waiting for transfers between devices  277 us (55%)
  matrix products  82.8 us (17%)
  Pallas kernels  31.1 us (6%)
  local copies, waits for them, and re-layouts  25.6 us (5%)
  between operations  22.4 us (4%)
  other arithmetic  21.7 us (4%)
  starting transfers between devices  15.5 us (3%)
  blocking collectives  15.4 us (3%)
    psum x4, waiting for transfers between devices, share_strips(): top_strip = lax.psum(row_strip, 'row')  136 us
    ppermute x8, waiting for transfers between devices, exchange_broadcast(): received = lax.ppermute(block, axis, partner)  77.6 us
    all_to_all x1, waiting for transfers between devices, body(): lax.all_to_all(payload, ('front', 'column', 'row'), split_axis=0, concat_...  63.7 us
    dot_general x4, matrix products, body(): jnp.dot(left_strip, top_strip, precision=HIGHEST, preferred_element_type=...  49 us
    pallas_call x1, Pallas kernels, scatter_tiles(): pl.pallas_call(assemble_kernel, out_shape=jax.ShapeDtypeStruct((local_row...  24.9 us
    unnamed x1, blocking collectives  15.4 us
    dot_general x3, matrix products, body(): jnp.dot(left_part, top_strip, precision=HIGHEST, preferred_element_type=j...  14 us
    unnamed x27, local copies, waits for them, and re-layouts  12.8 us
  transfers between devices with their start and end apart: 13, of which 12 were waited for; matrix products, arithmetic and copies ran while one was open for 12% of the time, Pallas kernels for 0%

profile of v1, /device:TPU:0, one launch (start us, length us, event | category | flops | bytes accessed | tf_op | source)
XLA Modules:
  0.0 492.0 jit_solution(1024511812281314377)
XLA Ops:
  9.2 1.2 scatter_custom_fusion.sources_ref
  10.4 6.2 %shard_map.73 = f32[64,128,128]{2,1,0:T(8,128)} custom-call(s32[64]{0:T(128)} %scatter_custom_fusion.sources_ref, f32[1,2,512,512]{3,2,1,0:T(8,128)} %blocks_ref.1), custom_call_target="tpu_custom_call" | custom-call | tf_op jit(solution)/shard_map/pallas_call | solution.py:77
  16.6 7.1 %all-to-all-start = ((f32[32,2,128,128]{3,2,1,0:T(8,128)}), f32[32,2,128,128]{3,2,1,0:T(8,128)}, u32[]{:S(2)}, u32[]{:S(2)}) async-start(f32[32,2,128,128]{3,2,1,0:T(8,128)} %bitcast.144), calls=%async_computation | async-start | bytes 8388608 | tf_op jit(solution)/shard_map/all_to_all | solution.py:216
  28.6 15.4 %all-reduce = s32[132]{0:T(256)S(1)} all-reduce(s32[132]{0:T(256)S(1)} %add_dynamic-update-slice_fusion), channel_id=2, replica_groups=mesh['front'=2,'column'=4,'row'=4] {'front'}, use_global_device_ids=true, to_apply=%add | all-reduce | flops 132 | bytes 1056
  49.3 1.2 copy.73.diag_ref
  50.5 63.7 %all-to-all-done = f32[32,2,128,128]{3,2,1,0:T(8,128)} async-done(((f32[32,2,128,128]{3,2,1,0:T(8,128)}), f32[32,2,128,128]{3,2,1,0:T(8,128)}, u32[]{:S(2)}, u32[]{:S(2)}) %all-to-all-start) | async-done | bytes 4194336 | tf_op jit(solution)/shard_map/all_to_all | solution.py:216
  114.2 24.9 %shard_map.74 = f32[1536,1536]{1,0:T(8,128)} custom-call(s32[64]{0:T(128)} %reshape.602.spots_ref, s32[1]{0:T(128)} %bitcast.16.offset_ref, f32[1536,1]{1,0:T(8,128)} %copy.73.diag_ref, f32[64,128,128]{2,1,0:T(8,128)} %bitcast.25.payload_ref), custom_call_target="tpu_custom_call" | custom-call | tf_op jit(solution)/shard_map/pallas_call | solution.py:117
  139.2 2.7 dynamic-slice_select_fusion
  141.8 3.2 constant_dynamic-slice_fusion.2
  145.1 2.4 fusion.15
  147.5 1.8 collective-permute-start
  149.2 3.2 collective-permute-done
  152.7 1.5 collective-permute-start.1
  156.3 33.1 %collective-permute-done.1 = f32[1536,256]{1,0:T(8,128)} collective-permute-done((f32[1536,256]{1,0:T(8,128)S(1)}, f32[1536,256]{1,0:T(8,128)}, u32[]{:S(2)}, u32[]{:S(2)}) %collective-permute-start.1) | collective-permute-done | bytes 1572896 | tf_op jit(solution)/shard_map/ppermute | solution.py:31
  189.3 1.7 broadcast_select_fusion.7
  191.1 33.1 %all-reduce.6.cloned.1.call-done = f32[256,1536]{1,0:T(8,128)} async-done(((f32[256,1536]{1,0:T(8,128)}), f32[256,1536]{1,0:T(8,128)}) %all-reduce.6.cloned.1.call-update) | async-done | bytes 1572880 | tf_op jit(solution)/shard_map/psum | solution.py:263
  224.1 4.7 fusion.8
  228.8 2.9 fusion.6
  231.7 3.5 fusion.13
  238.9 1.6 broadcast_select_fusion.4
  240.6 1.5 collective-permute-start.3
  242.1 11.7 %subtract_select_fusion.3 = f32[1536,1536]{1,0:T(8,128)S(1)} fusion(f32[1536,1536]{1,0:T(8,128)} %shard_map.74, f32[1536,256]{1,0:T(8,128)S(1)} %broadcast_select_fusion.7, f32[256,1536]{1,0:T(8,128)S(1)} %copy-done.4, pred[1536]{0:T(1024)(128)(4,1)S(1)} %get-tuple-element.52, pred[1536]{0:T(1024)(128)(4,1)S(1)} %get-tuple-element.53), kind=kOutput, calls=%fused_computation.6 | convolution fusion | flops 7254835200 | bytes 22023168 | tf_op jit(solution)/shard_map/dot_general | solution.py:302
  254.4 3.7 copy-done.2
  258.1 1.3 constant_dynamic-slice_fusion.1
  259.4 17.7 %collective-permute-done.3 = f32[1536,256]{1,0:T(8,128)S(1)} collective-permute-done((f32[1536,256]{1,0:T(8,128)S(1)}, f32[1536,256]{1,0:T(8,128)S(1)}, u32[]{:S(2)}, u32[]{:S(2)}) %collective-permute-start.3) | collective-permute-done | bytes 1572896 | tf_op jit(solution)/shard_map/ppermute | solution.py:31
  277.3 29.2 %all-reduce.8.cloned.1.call-done = f32[256,1536]{1,0:T(8,128)} async-done(((f32[256,1536]{1,0:T(8,128)}), f32[256,1536]{1,0:T(8,128)}) %all-reduce.8.cloned.1.call-update) | async-done | bytes 1572880 | tf_op jit(solution)/shard_map/psum | solution.py:263
  306.5 4.7 fusion.5
  311.2 2.9 fusion.3
  314.1 3.5 fusion.11
  319.8 1.5 collective-permute-done.4
  321.3 1.6 broadcast_select_fusion.2
  322.9 1.5 collective-permute-start.5
  324.5 11.6 %subtract_select_fusion.2 = f32[1536,1536]{1,0:T(8,128)S(1)} fusion(f32[1536,1536]{1,0:T(8,128)} %copy-done.2, f32[1536,256]{1,0:T(8,128)S(1)} %broadcast_select_fusion.5, f32[256,1536]{1,0:T(8,128)S(1)} %copy-done.5, pred[1536]{0:T(1024)(128)(4,1)S(1)} %get-tuple-element.28, pred[1536]{0:T(1024)(128)(4,1)S(1)} %get-tuple-element.27), kind=kOutput, calls=%fused_computation.5 | convolution fusion | flops 7254835200 | bytes 22023168 | tf_op jit(solution)/shard_map/dot_general | solution.py:302
  336.6 3.7 copy-done.3
  340.5 19.0 %collective-permute-done.5 = f32[1536,256]{1,0:T(8,128)S(1)} collective-permute-done((f32[1536,256]{1,0:T(8,128)S(1)}, f32[1536,256]{1,0:T(8,128)S(1)}, u32[]{:S(2)}, u32[]{:S(2)}) %collective-permute-start.5) | collective-permute-done | bytes 1572896 | tf_op jit(solution)/shard_map/ppermute | solution.py:31
  359.6 28.4 %all-reduce.10.cloned.1.call-done = f32[256,1536]{1,0:T(8,128)} async-done(((f32[256,1536]{1,0:T(8,128)}), f32[256,1536]{1,0:T(8,128)}) %all-reduce.10.cloned.1.call-update) | async-done | bytes 1572880 | tf_op jit(solution)/shard_map/psum | solution.py:263
  388.0 4.6 fusion.2
  392.6 2.4 fusion
  395.0 2.4 fusion.9
  398.5 2.5 collective-permute-done.6
  401.0 1.7 broadcast_select_fusion
  402.7 1.4 collective-permute-start.7
  404.3 13.4 %subtract_select_fusion.1 = f32[1536,1536]{1,0:T(8,128)} fusion(f32[1536,1536]{1,0:T(8,128)} %copy-done.3, f32[1536,256]{1,0:T(8,128)S(1)} %broadcast_select_fusion.3, f32[256,1536]{1,0:T(8,128)} %all-reduce.10.cloned.1.call-done, pred[1536]{0:T(1024)(128)(4,1)S(1)} %get-tuple-element.26, pred[1536]{0:T(1024)(128)(4,1)S(1)} %get-tuple-element.25), kind=kOutput, calls=%fused_computation.4 | convolution fusion | flops 7254835200 | bytes 22023168 | tf_op jit(solution)/shard_map/dot_general | solution.py:302
  417.7 2.9 select_dynamic-update-slice_fusion
  420.7 45.3 %all-reduce.12.cloned.1.call-done = f32[256,1536]{1,0:T(8,128)} async-done(((f32[256,1536]{1,0:T(8,128)}), f32[256,1536]{1,0:T(8,128)}) %all-reduce.12.cloned.1.call-update) | async-done | bytes 1572880 | tf_op jit(solution)/shard_map/psum | solution.py:263
  466.0 12.3 %subtract_select_fusion = f32[1536,1536]{1,0:T(8,128)S(1)} fusion(f32[1536,1536]{1,0:T(8,128)} %select_dynamic-update-slice_fusion, f32[256,1536]{1,0:T(8,128)} %all-reduce.12.cloned.1.call-done, pred[1536]{0:T(1024)(128)(4,1)S(1)} %get-tuple-element.24, pred[1536]{0:T(1024)(128)(4,1)S(1)} %get-tuple-element.23, f32[1536,256]{1,0:T(8,128)} %collective-permute-done.7, ...), kind=kOutput, calls=%fused_computation.3 | convolution fusion | flops 7255228416 | bytes 23596032 | tf_op jit(solution)/shard_map/dot_general | solution.py:302
  478.3 3.7 copy.82
  482.0 3.0 bitcast_dynamic-update-slice_fusion
  (128 shorter events, 15.3 us)
Async XLA Ops:
  6.5 42.8 %copy-start = (f32[1,6144]{1,0:T(1,128)S(1)}, f32[1,6144]{1,0:T(1,128)}, u32[]{:S(2)}) copy-start(f32[1,6144]{1,0:T(1,128)} %param.11) | copy-start | bytes 73732
  16.6 7.2 %copy-start.9 = (s32[1,2,16]{2,1,0:T(2,128)S(1)}, s32[1,2,16]{2,1,0:T(2,128)}, u32[]{:S(2)}) copy-start(s32[1,2,16]{2,1,0:T(2,128)} %param.8) | copy-start | bytes 388
  16.6 7.3 %copy-start.10 = (s32[1,2,16]{2,1,0:T(2,128)S(1)}, s32[1,2,16]{2,1,0:T(2,128)}, u32[]{:S(2)}) copy-start(s32[1,2,16]{2,1,0:T(2,128)} %param.9) | copy-start | bytes 388
  16.6 7.4 %copy-start.7 = (s32[1,4]{1,0:T(1,128)S(1)}, s32[1,4]{1,0:T(1,128)}, u32[]{:S(2)}) copy-start(s32[1,4]{1,0:T(1,128)} %param.12) | copy-start | bytes 52
  16.6 10.6 %copy-start.11 = (u32[32]{0:T(128)S(1)}, u32[32]{0:T(128)}, u32[]{:S(2)}) copy-start(u32[32]{0:T(128)} %constant.349) | copy-start | bytes 388
  16.6 11.8 %copy-start.8 = (s32[1,2]{1,0:T(1,128)S(1)}, s32[1,2]{1,0:T(1,128)}, u32[]{:S(2)}) copy-start(s32[1,2]{1,0:T(1,128)} %param.10) | copy-start | bytes 28
  16.6 97.6 %all-to-all-start = ((f32[32,2,128,128]{3,2,1,0:T(8,128)}), f32[32,2,128,128]{3,2,1,0:T(8,128)}, u32[]{:S(2)}, u32[]{:S(2)}) async-start(f32[32,2,128,128]{3,2,1,0:T(8,128)} %bitcast.144), calls=%async_computation | async-start | bytes 8388608 | tf_op jit(solution)/shard_map/all_to_all | solution.py:216
  23.7 200.4 %all-reduce.6.cloned.1.call-start = ((), (), s32[]{:S(2)}) async-start(), calls=%async_computation.1 | async-start | bytes 3145728 | tf_op jit(solution)/shard_map/psum | solution.py:263
  147.5 4.9 %collective-permute-start = (f32[1536,256]{1,0:T(8,128)S(1)}, f32[1536,256]{1,0:T(8,128)}, u32[]{:S(2)}, u32[]{:S(2)}) collective-permute-start(f32[1536,256]{1,0:T(8,128)S(1)} %fusion.15), channel_id=1, source_target_pairs={{0,4},{4,0},{8,12},{12,8},{1,5},{5,1},{9,13},{13,9},{2,6},{6,2},{1... | collective-permute-start | bytes 4718600 | tf_op jit(solution)/shard_map/ppermute | solution.py:31
  152.7 36.7 %collective-permute-start.1 = (f32[1536,256]{1,0:T(8,128)S(1)}, f32[1536,256]{1,0:T(8,128)}, u32[]{:S(2)}, u32[]{:S(2)}) collective-permute-start(f32[1536,256]{1,0:T(8,128)S(1)} %broadcast_select_fusion.6), channel_id=1, source_target_pairs={{0,8},{4,12},{8,0},{12,4},{1,9},{5,13},{9,1},{13,5},{2,10},{6,14},... | collective-permute-start | bytes 4718600 | tf_op jit(solution)/shard_map/ppermute | solution.py:31
  154.2 152.3 %all-reduce.8.cloned.1.call-start = ((), (), s32[]{:S(2)}) async-start(), calls=%async_computation.2 | async-start | bytes 3145728 | tf_op jit(solution)/shard_map/psum | solution.py:263
  224.1 4.7 copy-start.4
  235.2 3.8 collective-permute-start.2
  238.0 150.0 %all-reduce.10.cloned.1.call-start = ((), (), s32[]{:S(2)}) async-start(), calls=%async_computation.3 | async-start | bytes 3145728 | tf_op jit(solution)/shard_map/psum | solution.py:263
  240.6 36.5 %collective-permute-start.3 = (f32[1536,256]{1,0:T(8,128)S(1)}, f32[1536,256]{1,0:T(8,128)S(1)}, u32[]{:S(2)}, u32[]{:S(2)}) collective-permute-start(f32[1536,256]{1,0:T(8,128)S(1)} %broadcast_select_fusion.4), channel_id=1, source_target_pairs={{0,8},{4,12},{8,0},{12,4},{1,9},{5,13},{9,1},{13,5},{2,10},{6,14},... | collective-permute-start | bytes 4718600 | tf_op jit(solution)/shard_map/ppermute | solution.py:31
  254.3 3.7 copy-start.2
  306.5 4.7 copy-start.5
  317.6 3.8 collective-permute-start.4
  319.5 146.5 %all-reduce.12.cloned.1.call-start = ((), (), s32[]{:S(2)}) async-start(), calls=%async_computation.4 | async-start | bytes 3145728 | tf_op jit(solution)/shard_map/psum | solution.py:263
  322.9 36.5 %collective-permute-start.5 = (f32[1536,256]{1,0:T(8,128)S(1)}, f32[1536,256]{1,0:T(8,128)S(1)}, u32[]{:S(2)}, u32[]{:S(2)}) collective-permute-start(f32[1536,256]{1,0:T(8,128)S(1)} %broadcast_select_fusion.2), channel_id=1, source_target_pairs={{0,8},{4,12},{8,0},{12,4},{1,9},{5,13},{9,1},{13,5},{2,10},{6,14},... | collective-permute-start | bytes 4718600 | tf_op jit(solution)/shard_map/ppermute | solution.py:31
  336.5 3.7 copy-start.3
  397.4 1.1 copy-start.6
  397.4 3.6 collective-permute-start.6
  402.7 63.2 %collective-permute-start.7 = (f32[1536,256]{1,0:T(8,128)S(1)}, f32[1536,256]{1,0:T(8,128)}, u32[]{:S(2)}, u32[]{:S(2)}) collective-permute-start(f32[1536,256]{1,0:T(8,128)S(1)} %broadcast_select_fusion), channel_id=1, source_target_pairs={{0,8},{4,12},{8,0},{12,4},{1,9},{5,13},{9,1},{13,5},{2,10},{6,14},... | collective-permute-start | bytes 4718600 | tf_op jit(solution)/shard_map/ppermute | solution.py:31
  482.0 3.0 copy-start.1
Sparse Core Ops, SparseCore 0:
  154.3 69.7 all-reduce.5
  238.1 68.3 all-reduce.7
  319.6 68.3 all-reduce.9
  397.6 68.2 all-reduce.11

commit v2 on v0

--- a/solution.py
+++ b/solution.py
@@ -305,23 +305,23 @@
             left_next, top_next = share_strips(next_col, next_row, step_index + 1)
         eliminate_matrix = matrix
         eliminate_active_rows, eliminate_active_cols = actives(step_index)
+        eliminate_col_owner, eliminate_row_owner, eliminate_col_offset, eliminate_row_offset = (
+            strip_bounds(step_index)
+        )
+        present = lax.dynamic_slice_in_dim(eliminate_matrix, eliminate_col_offset, PANEL, 1)
+        fresh_col = jnp.where(
+            (col_id == eliminate_col_owner) & eliminate_active_rows[:, None], left_strip, present
+        )
+        eliminate_matrix = lax.dynamic_update_slice_in_dim(
+            eliminate_matrix, fresh_col, eliminate_col_offset, 1
+        )
         product = jnp.dot(
             left_strip, top_strip, precision=HIGHEST, preferred_element_type=jnp.float32
         )
-        eliminate_matrix = jnp.where(
+        matrix = jnp.where(
             eliminate_active_rows[:, None] & eliminate_active_cols[None, :],
             eliminate_matrix - product,
             eliminate_matrix,
-        )
-        eliminate_col_owner, eliminate_row_owner, eliminate_col_offset, eliminate_row_offset = (
-            strip_bounds(step_index)
-        )
-        present = lax.dynamic_slice_in_dim(eliminate_matrix, eliminate_col_offset, PANEL, 1)
-        fresh_col = jnp.where(
-            (col_id == eliminate_col_owner) & eliminate_active_rows[:, None], left_strip, present
-        )
-        matrix = lax.dynamic_update_slice_in_dim(
-            eliminate_matrix, fresh_col, eliminate_col_offset, 1
         )
         if step_index + 1 < PANELS:
             left_strip, top_strip = (left_next, top_next)

time: 482 us -> 490 us (1.017)
  other arithmetic: 21.7 us -> 33.2 us
  waiting for transfers between devices: 272 us -> 263 us
  local copies, waits for them, and re-layouts: 25 us -> 31 us
    psum x4, waiting for transfers between devices: 139 us -> 118 us  [share_strips(): top_strip = lax.psum(row_strip, 'row')]
    ppermute x8, waiting for transfers between devices: 69.1 us -> 80.8 us  [exchange_broadcast(): received = lax.ppermute(block, axis, partner)]
    dynamic_update_slice x4, other arithmetic: 5.45 us -> 16.2 us  [body(): lax.dynamic_update_slice_in_dim(eliminate_matrix, fresh_col, eliminate_co...]
    unnamed x27 -> x29, local copies, waits for them, and re-layouts: 12.8 us -> 23 us
  transfers between devices with their start and end apart: 13 -> 13, of which waited for: 12 -> 13; matrix products, arithmetic and copies ran while one was open for 14% -> 17% of each run, Pallas kernels for 0% -> 0%
where the time goes in v2:
time: 490 us; the launch traced here: 484 us
  waiting for transfers between devices  263 us (54%)
  matrix products  85.4 us (17%)
  other arithmetic  33.2 us (7%)
  local copies, waits for them, and re-layouts  31 us (6%)
  between operations  22.2 us (5%)
  blocking collectives  17.4 us (4%)
  Pallas kernels  16 us (3%)
  starting transfers between devices  16 us (3%)
    psum x4, waiting for transfers between devices, share_strips(): top_strip = lax.psum(row_strip, 'row')  118 us
    ppermute x8, waiting for transfers between devices, exchange_broadcast(): received = lax.ppermute(block, axis, partner)  80.8 us
    all_to_all x1, waiting for transfers between devices, body(): lax.all_to_all(payload, ('front', 'column', 'row'), split_axis=0, concat_...  63.8 us
    dot_general x4, matrix products, body(): jnp.dot(left_strip, top_strip, precision=HIGHEST, preferred_element_type=...  51.1 us
    unnamed x29, local copies, waits for them, and re-layouts  23 us
    unnamed x1, blocking collectives  17.4 us
    dynamic_update_slice x4, other arithmetic, body(): lax.dynamic_update_slice_in_dim(eliminate_matrix, fresh_col, eliminate_co...  16.2 us
    dot_general x3, matrix products, body(): jnp.dot(left_part, top_strip, precision=HIGHEST, preferred_element_type=j...  14 us
  transfers between devices with their start and end apart: 13, of which 13 were waited for; matrix products, arithmetic and copies ran while one was open for 17% of the time, Pallas kernels for 0%

profile of v2, /device:TPU:0, one launch (start us, length us, event | category | flops | bytes accessed | tf_op | source)
XLA Modules:
  0.0 484.3 jit_solution(11584961151610496195)
XLA Ops:
  10.4 6.2 %shard_map.73 = f32[64,128,128]{2,1,0:T(8,128)} custom-call(s32[64]{0:T(128)} %scatter_custom_fusion.sources_ref, f32[1,2,512,512]{3,2,1,0:T(8,128)} %blocks_ref.1), custom_call_target="tpu_custom_call" | custom-call | tf_op jit(solution)/shard_map/pallas_call | solution.py:77
  16.6 7.1 %all-to-all-start = ((f32[32,2,128,128]{3,2,1,0:T(8,128)}), f32[32,2,128,128]{3,2,1,0:T(8,128)}, u32[]{:S(2)}, u32[]{:S(2)}) async-start(f32[32,2,128,128]{3,2,1,0:T(8,128)} %bitcast.140), calls=%async_computation | async-start | bytes 8388608 | tf_op jit(solution)/shard_map/all_to_all | solution.py:224
  26.6 17.4 %all-reduce = s32[132]{0:T(256)S(1)} all-reduce(s32[132]{0:T(256)S(1)} %add_dynamic-update-slice_fusion), channel_id=2, replica_groups=mesh['front'=2,'column'=4,'row'=4] {'front'}, use_global_device_ids=true, to_apply=%add | all-reduce | flops 132 | bytes 1056
  50.4 63.8 %all-to-all-done = f32[32,2,128,128]{3,2,1,0:T(8,128)} async-done(((f32[32,2,128,128]{3,2,1,0:T(8,128)}), f32[32,2,128,128]{3,2,1,0:T(8,128)}, u32[]{:S(2)}, u32[]{:S(2)}) %all-to-all-start) | async-done | bytes 4194336 | tf_op jit(solution)/shard_map/all_to_all | solution.py:224
  114.2 9.9 %shard_map.74 = f32[1536,1536]{1,0:T(8,128)} custom-call(s32[64]{0:T(128)} %reshape.600.spots_ref, s32[1]{0:T(128)} %bitcast.16.offset_ref, f32[1536,1]{1,0:T(8,128)} %copy.73.diag_ref, f32[64,128,128]{2,1,0:T(8,128)} %bitcast.25.payload_ref), custom_call_target="tpu_custom_call" | custom-call | tf_op jit(solution)/shard_map/pallas_call | solution.py:125
  124.1 2.9 fusion.10
  126.9 1.7 collective-permute-start
  130.0 1.9 collective-permute-done
  131.9 1.7 broadcast_select_fusion.6
  133.6 1.5 collective-permute-start.1
  135.1 2.6 dynamic-slice_select_fusion
  142.3 8.3 %copy.75 = f32[1536,1536]{1,0:T(8,128)} copy(f32[1536,1536]{1,0:T(8,128)} %shard_map.74) | data formatting | bytes 18874368
  150.6 18.4 %collective-permute-done.1 = f32[1536,256]{1,0:T(8,128)} collective-permute-done((f32[1536,256]{1,0:T(8,128)S(1)}, f32[1536,256]{1,0:T(8,128)}, u32[]{:S(2)}, u32[]{:S(2)}) %collective-permute-start.1) | collective-permute-done | bytes 1572896 | tf_op jit(solution)/shard_map/ppermute | solution.py:31
  169.0 4.7 select_dynamic-update-slice_fusion.3
  173.7 32.9 %all-reduce.6.cloned.1.call-done = f32[256,1536]{1,0:T(8,128)} async-done(((f32[256,1536]{1,0:T(8,128)}), f32[256,1536]{1,0:T(8,128)}) %all-reduce.6.cloned.1.call-update) | async-done | bytes 1572880 | tf_op jit(solution)/shard_map/psum | solution.py:271
  206.6 4.7 fusion.9
  211.3 2.9 fusion.7
  214.1 3.5 fusion.16
  217.6 3.7 collective-permute-done.2
  221.4 2.7 broadcast_select_fusion.4
  228.0 11.8 %subtract_select_fusion.3 = f32[1536,1536]{1,0:T(8,128)S(1)} fusion(f32[1536,1536]{1,0:T(8,128)} %get-tuple-element.29, f32[1536,256]{1,0:T(8,128)S(1)} %get-tuple-element.30, f32[256,1536]{1,0:T(8,128)S(1)} %copy-done.4, pred[1536]{0:T(1024)(128)(4,1)S(1)} %broadcast_compare_fusion.1, pred[1536]{0:T(1024)(128)(4,1)S(1)} %broadcast_compare_fusion.2), kind=kOutput, calls=%fused_computation.6 | convolution fusion | flops 7254835200 | bytes 22023168 | tf_op jit(solution)/shard_map/dot_general | solution.py:318
  239.8 3.8 copy.77
  243.6 2.7 copy-done.2
  246.3 14.5 %collective-permute-done.3 = f32[1536,256]{1,0:T(8,128)} collective-permute-done((f32[1536,256]{1,0:T(8,128)}, f32[1536,256]{1,0:T(8,128)}, u32[]{:S(2)}, u32[]{:S(2)}) %collective-permute-start.3) | collective-permute-done | bytes 1572896 | tf_op jit(solution)/shard_map/ppermute | solution.py:31
  260.9 4.5 select_dynamic-update-slice_fusion.2
  265.4 27.8 %all-reduce.8.cloned.1.call-done = f32[256,1536]{1,0:T(8,128)} async-done(((f32[256,1536]{1,0:T(8,128)}), f32[256,1536]{1,0:T(8,128)}) %all-reduce.8.cloned.1.call-update) | async-done | bytes 1572880 | tf_op jit(solution)/shard_map/psum | solution.py:271
  293.2 4.7 fusion.6
  297.9 2.9 fusion.4
  300.8 3.5 fusion.14
  304.3 3.7 collective-permute-done.4
  308.0 2.7 broadcast_select_fusion.2
  314.6 11.8 %subtract_select_fusion.2 = f32[1536,1536]{1,0:T(8,128)S(1)} fusion(f32[1536,1536]{1,0:T(8,128)} %get-tuple-element.27, f32[1536,256]{1,0:T(8,128)S(1)} %get-tuple-element.28, f32[256,1536]{1,0:T(8,128)S(1)} %copy-done.5, pred[1536]{0:T(1024)(128)(4,1)S(1)} %get-tuple-element.23, pred[1536]{0:T(1024)(128)(4,1)S(1)} %get-tuple-element.24), kind=kOutput, calls=%fused_computation.5 | convolution fusion | flops 7254835200 | bytes 22023168 | tf_op jit(solution)/shard_map/dot_general | solution.py:318
  326.5 3.8 copy.79
  330.3 2.7 copy-done.3
  333.0 14.5 %collective-permute-done.5 = f32[1536,256]{1,0:T(8,128)} collective-permute-done((f32[1536,256]{1,0:T(8,128)}, f32[1536,256]{1,0:T(8,128)}, u32[]{:S(2)}, u32[]{:S(2)}) %collective-permute-start.5) | collective-permute-done | bytes 1572896 | tf_op jit(solution)/shard_map/ppermute | solution.py:31
  347.5 4.0 select_dynamic-update-slice_fusion.1
  351.5 28.3 %all-reduce.10.cloned.1.call-done = f32[256,1536]{1,0:T(8,128)} async-done(((f32[256,1536]{1,0:T(8,128)}), f32[256,1536]{1,0:T(8,128)}) %all-reduce.10.cloned.1.call-update) | async-done | bytes 1572880 | tf_op jit(solution)/shard_map/psum | solution.py:271
  379.8 4.6 fusion.3
  384.4 2.4 fusion.1
  386.8 2.4 fusion.12
  390.3 2.5 collective-permute-done.6
  392.8 1.6 broadcast_select_fusion
  394.4 1.5 collective-permute-start.7
  396.1 13.4 %subtract_select_fusion.1 = f32[1536,1536]{1,0:T(8,128)} fusion(f32[1536,1536]{1,0:T(8,128)} %get-tuple-element.25, f32[1536,256]{1,0:T(8,128)S(1)} %get-tuple-element.26, f32[256,1536]{1,0:T(8,128)} %all-reduce.10.cloned.1.call-done, pred[1536]{0:T(1024)(128)(4,1)S(1)} %get-tuple-element.21, pred[1536]{0:T(1024)(128)(4,1)S(1)} %get-tuple-element.22), kind=kOutput, calls=%fused_computation.4 | convolution fusion | flops 7254835200 | bytes 22023168 | tf_op jit(solution)/shard_map/dot_general | solution.py:318
  409.5 21.5 %collective-permute-done.7 = f32[1536,256]{1,0:T(8,128)} collective-permute-done((f32[1536,256]{1,0:T(8,128)S(1)}, f32[1536,256]{1,0:T(8,128)}, u32[]{:S(2)}, u32[]{:S(2)}) %collective-permute-start.7) | collective-permute-done | bytes 1572896 | tf_op jit(solution)/shard_map/ppermute | solution.py:31
  431.0 3.0 select_dynamic-update-slice_fusion
  434.0 29.5 %all-reduce.12.cloned.1.call-done = f32[256,1536]{1,0:T(8,128)} async-done(((f32[256,1536]{1,0:T(8,128)}), f32[256,1536]{1,0:T(8,128)}) %all-reduce.12.cloned.1.call-update) | async-done | bytes 1572880 | tf_op jit(solution)/shard_map/psum | solution.py:271
  463.5 14.0 %fusion = f32[1,1536,1536]{2,1,0:T(8,128)} fusion(f32[1536,1536]{1,0:T(8,128)} %select_dynamic-update-slice_fusion, f32[256,1536]{1,0:T(8,128)} %all-reduce.12.cloned.1.call-done, pred[1536]{0:T(1024)(128)(4,1)S(1)} %get-tuple-element.19, pred[1536]{0:T(1024)(128)(4,1)S(1)} %get-tuple-element.20, f32[1536,256]{1,0:T(8,128)} %collective-permute-done.7, ...), kind=kOutput, calls=%fused_computation.7 | convolution fusion | flops 7255228416 | bytes 23596032 | tf_op jit(solution)/shard_map/dot_general | solution.py:318
  (125 shorter events, 19.3 us)
Async XLA Ops:
  6.5 42.7 %copy-start = (f32[1,6144]{1,0:T(1,128)S(1)}, f32[1,6144]{1,0:T(1,128)}, u32[]{:S(2)}) copy-start(f32[1,6144]{1,0:T(1,128)} %param.11) | copy-start | bytes 73732
  16.6 7.2 %copy-start.9 = (s32[1,2,16]{2,1,0:T(2,128)S(1)}, s32[1,2,16]{2,1,0:T(2,128)}, u32[]{:S(2)}) copy-start(s32[1,2,16]{2,1,0:T(2,128)} %param.8) | copy-start | bytes 388
  16.6 7.3 %copy-start.10 = (s32[1,2,16]{2,1,0:T(2,128)S(1)}, s32[1,2,16]{2,1,0:T(2,128)}, u32[]{:S(2)}) copy-start(s32[1,2,16]{2,1,0:T(2,128)} %param.9) | copy-start | bytes 388
  16.6 7.4 %copy-start.7 = (s32[1,4]{1,0:T(1,128)S(1)}, s32[1,4]{1,0:T(1,128)}, u32[]{:S(2)}) copy-start(s32[1,4]{1,0:T(1,128)} %param.12) | copy-start | bytes 52
  16.6 8.7 %copy-start.11 = (u32[32]{0:T(128)S(1)}, u32[32]{0:T(128)}, u32[]{:S(2)}) copy-start(u32[32]{0:T(128)} %constant.348) | copy-start | bytes 388
  16.6 9.9 %copy-start.8 = (s32[1,2]{1,0:T(1,128)S(1)}, s32[1,2]{1,0:T(1,128)}, u32[]{:S(2)}) copy-start(s32[1,2]{1,0:T(1,128)} %param.10) | copy-start | bytes 28
  16.6 97.6 %all-to-all-start = ((f32[32,2,128,128]{3,2,1,0:T(8,128)}), f32[32,2,128,128]{3,2,1,0:T(8,128)}, u32[]{:S(2)}, u32[]{:S(2)}) async-start(f32[32,2,128,128]{3,2,1,0:T(8,128)} %bitcast.140), calls=%async_computation | async-start | bytes 8388608 | tf_op jit(solution)/shard_map/all_to_all | solution.py:224
  23.7 182.9 %all-reduce.6.cloned.1.call-start = ((), (), s32[]{:S(2)}) async-start(), calls=%async_computation.1 | async-start | bytes 3145728 | tf_op jit(solution)/shard_map/psum | solution.py:271
  126.9 4.9 %collective-permute-start = (f32[1536,256]{1,0:T(8,128)S(1)}, f32[1536,256]{1,0:T(8,128)}, u32[]{:S(2)}, u32[]{:S(2)}) collective-permute-start(f32[1536,256]{1,0:T(8,128)S(1)} %fusion.10), channel_id=1, source_target_pairs={{0,4},{4,0},{8,12},{12,8},{1,5},{5,1},{9,13},{13,9},{2,6},{6,2},{1... | collective-permute-start | bytes 4718600 | tf_op jit(solution)/shard_map/ppermute | solution.py:31
  133.6 35.4 %collective-permute-start.1 = (f32[1536,256]{1,0:T(8,128)S(1)}, f32[1536,256]{1,0:T(8,128)}, u32[]{:S(2)}, u32[]{:S(2)}) collective-permute-start(f32[1536,256]{1,0:T(8,128)S(1)} %broadcast_select_fusion.6), channel_id=1, source_target_pairs={{0,8},{4,12},{8,0},{12,4},{1,9},{5,13},{9,1},{13,5},{2,10},{6,14},... | collective-permute-start | bytes 4718600 | tf_op jit(solution)/shard_map/ppermute | solution.py:31
  137.8 155.4 %all-reduce.8.cloned.1.call-start = ((), (), s32[]{:S(2)}) async-start(), calls=%async_computation.2 | async-start | bytes 3145728 | tf_op jit(solution)/shard_map/psum | solution.py:271
  206.6 4.7 copy-start.4
  217.6 3.8 collective-permute-start.2
  224.1 36.8 %collective-permute-start.3 = (f32[1536,256]{1,0:T(8,128)}, f32[1536,256]{1,0:T(8,128)}, u32[]{:S(2)}, u32[]{:S(2)}) collective-permute-start(f32[1536,256]{1,0:T(8,128)} %broadcast_select_fusion.4), channel_id=1, source_target_pairs={{0,8},{4,12},{8,0},{12,4},{1,9},{5,13},{9,1},{13,5},{2,10},{6,14},... | collective-permute-start | bytes 4718600 | tf_op jit(solution)/shard_map/ppermute | solution.py:31
  225.8 154.0 %all-reduce.10.cloned.1.call-start = ((), (), s32[]{:S(2)}) async-start(), calls=%async_computation.3 | async-start | bytes 3145728 | tf_op jit(solution)/shard_map/psum | solution.py:271
  239.8 6.5 %copy-start.2 = (f32[1536,1536]{1,0:T(8,128)}, f32[1536,1536]{1,0:T(8,128)S(1)}, u32[]{:S(2)}) copy-start(f32[1536,1536]{1,0:T(8,128)S(1)} %subtract_select_fusion.3) | copy-start | bytes 28311556
  293.2 4.7 copy-start.5
  304.2 3.8 collective-permute-start.4
  310.8 36.8 %collective-permute-start.5 = (f32[1536,256]{1,0:T(8,128)}, f32[1536,256]{1,0:T(8,128)}, u32[]{:S(2)}, u32[]{:S(2)}) collective-permute-start(f32[1536,256]{1,0:T(8,128)} %broadcast_select_fusion.2), channel_id=1, source_target_pairs={{0,8},{4,12},{8,0},{12,4},{1,9},{5,13},{9,1},{13,5},{2,10},{6,14},... | collective-permute-start | bytes 4718600 | tf_op jit(solution)/shard_map/ppermute | solution.py:31
  312.4 151.1 %all-reduce.12.cloned.1.call-start = ((), (), s32[]{:S(2)}) async-start(), calls=%async_computation.4 | async-start | bytes 3145728 | tf_op jit(solution)/shard_map/psum | solution.py:271
  326.5 6.5 %copy-start.3 = (f32[1536,1536]{1,0:T(8,128)}, f32[1536,1536]{1,0:T(8,128)S(1)}, u32[]{:S(2)}) copy-start(f32[1536,1536]{1,0:T(8,128)S(1)} %subtract_select_fusion.2) | copy-start | bytes 28311556
  389.2 1.1 copy-start.6
  389.2 3.6 collective-permute-start.6
  394.4 36.6 %collective-permute-start.7 = (f32[1536,256]{1,0:T(8,128)S(1)}, f32[1536,256]{1,0:T(8,128)}, u32[]{:S(2)}, u32[]{:S(2)}) collective-permute-start(f32[1536,256]{1,0:T(8,128)S(1)} %broadcast_select_fusion), channel_id=1, source_target_pairs={{0,8},{4,12},{8,0},{12,4},{1,9},{5,13},{9,1},{13,5},{2,10},{6,14},... | collective-permute-start | bytes 4718600 | tf_op jit(solution)/shard_map/ppermute | solution.py:31
  463.5 14.0 %copy-start.1 = (f32[1,6144]{1,0:T(1,128)S(1)}, f32[1,6144]{1,0:T(1,128)}, u32[]{:S(2)}) copy-start(f32[1,6144]{1,0:T(1,128)} %param.11) | copy-start | bytes 73732
Sparse Core Ops, SparseCore 0:
  137.9 68.6 all-reduce.5
  225.9 67.2 all-reduce.7
  312.5 67.2 all-reduce.9
  396.2 67.2 all-reduce.11

commit v3 on v0

--- a/solution.py
+++ b/solution.py
@@ -146,8 +146,14 @@
     maps = jnp.concatenate(
         [row_map[0].reshape(-1), col_map[0].reshape(-1), child_size[0].reshape(-1)]
     )
-    every = lax.all_gather(maps, "front")
     front_id = lax.axis_index("front")
+    shifted = [maps] + [
+        lax.ppermute(maps, "front", [(i, (i + shift) % groups) for i in range(groups)])
+        for shift in range(1, groups)
+    ]
+    every = jnp.take(
+        jnp.stack(shifted), (front_id - jnp.arange(groups, dtype=jnp.int32)) % groups, axis=0
+    )
     row_maps = every[:, :span].reshape(groups, children, side)[:, front_id]
     col_maps = every[:, span : 2 * span].reshape(groups, children, side)[:, front_id]
     sizes = every[:, 2 * span :].reshape(groups, children)[:, front_id]

time: 482 us -> 483 us (level)
  waiting for transfers between devices: 272 us -> 291 us
  blocking collectives: 17.4 us -> 0 us
    unnamed x1 -> x0, blocking collectives: 17.4 us -> none
    ppermute x0 -> x1, waiting for transfers between devices: none -> 15.4 us  [arrival_labels(): lax.ppermute(maps, 'front', [(i, (i + shift) % groups) for i in range(gro...]
    unnamed x27 -> x23, local copies, waits for them, and re-layouts: 12.8 us -> 12.2 us
  transfers between devices with their start and end apart: 13 -> 14, of which waited for: 12 -> 13; matrix products, arithmetic and copies ran while one was open for 14% -> 13% of each run, Pallas kernels for 0% -> 0%
where the time goes in v3:
time: 483 us; the launch traced here: 474 us
  waiting for transfers between devices  291 us (60%)
  matrix products  83.4 us (17%)
  local copies, waits for them, and re-layouts  24.9 us (5%)
  between operations  21.7 us (4%)
  other arithmetic  20.4 us (4%)
  starting transfers between devices  17.3 us (4%)
  Pallas kernels  16.1 us (3%)
    psum x4, waiting for transfers between devices, share_strips(): top_strip = lax.psum(row_strip, 'row')  140 us
    ppermute x8, waiting for transfers between devices, exchange_broadcast(): received = lax.ppermute(block, axis, partner)  70.3 us
    all_to_all x1, waiting for transfers between devices, body(): lax.all_to_all(payload, ('front', 'column', 'row'), split_axis=0, concat_...  64.7 us
    dot_general x4, matrix products, body(): jnp.dot(left_strip, top_strip, precision=HIGHEST, preferred_element_type=...  49 us
    ppermute x1, waiting for transfers between devices, arrival_labels(): lax.ppermute(maps, 'front', [(i, (i + shift) % groups) for i in range(gro...  15.4 us
    dot_general x3, matrix products, body(): jnp.dot(left_part, top_strip, precision=HIGHEST, preferred_element_type=j...  14 us
    dot_general x4, matrix products, share_strips(): jnp.dot(col_strip, inverses[step_index], precision=HIGHEST, preferred_ele...  12.3 us
    unnamed x23, local copies, waits for them, and re-layouts  12.2 us
  transfers between devices with their start and end apart: 14, of which 13 were waited for; matrix products, arithmetic and copies ran while one was open for 13% of the time, Pallas kernels for 0%

profile of v3, /device:TPU:0, one launch (start us, length us, event | category | flops | bytes accessed | tf_op | source)
XLA Modules:
  0.0 474.5 jit_solution(10165916905087135874)
XLA Ops:
  9.2 1.2 scatter_custom_fusion.sources_ref
  10.4 6.1 %shard_map.73 = f32[64,128,128]{2,1,0:T(8,128)} custom-call(s32[64]{0:T(128)} %scatter_custom_fusion.sources_ref, f32[1,2,512,512]{3,2,1,0:T(8,128)} %blocks_ref.1), custom_call_target="tpu_custom_call" | custom-call | tf_op jit(solution)/shard_map/pallas_call | solution.py:77
  16.6 7.2 %all-to-all-start = ((f32[32,2,128,128]{3,2,1,0:T(8,128)}), f32[32,2,128,128]{3,2,1,0:T(8,128)}, u32[]{:S(2)}, u32[]{:S(2)}) async-start(f32[32,2,128,128]{3,2,1,0:T(8,128)} %bitcast.147), calls=%async_computation | async-start | bytes 8388608 | tf_op jit(solution)/shard_map/all_to_all | solution.py:230
  24.1 1.7 collective-permute-start
  27.5 1.2 copy.73.diag_ref
  28.7 15.4 %collective-permute-done = s32[66]{0:T(128)S(1)} collective-permute-done((s32[66]{0:T(128)S(1)}, s32[66]{0:T(128)S(1)}, u32[]{:S(2)}, u32[]{:S(2)}) %collective-permute-start) | collective-permute-done | bytes 296 | tf_op jit(solution)/shard_map/ppermute | solution.py:151
  49.6 64.7 %all-to-all-done = f32[32,2,128,128]{3,2,1,0:T(8,128)} async-done(((f32[32,2,128,128]{3,2,1,0:T(8,128)}), f32[32,2,128,128]{3,2,1,0:T(8,128)}, u32[]{:S(2)}, u32[]{:S(2)}) %all-to-all-start) | async-done | bytes 4194336 | tf_op jit(solution)/shard_map/all_to_all | solution.py:230
  114.3 9.9 %shard_map.74 = f32[1536,1536]{1,0:T(8,128)} custom-call(s32[64]{0:T(128)} %reshape.656.spots_ref, s32[1]{0:T(128)} %bitcast.18.offset_ref, f32[1536,1]{1,0:T(8,128)} %copy.73.diag_ref, f32[64,128,128]{2,1,0:T(8,128)} %bitcast.27.payload_ref), custom_call_target="tpu_custom_call" | custom-call | tf_op jit(solution)/shard_map/pallas_call | solution.py:125
  124.2 2.9 fusion.9
  127.2 1.7 collective-permute-start.1
  130.2 1.9 collective-permute-done.1
  132.3 1.5 collective-permute-start.2
  133.8 2.6 dynamic-slice_select_fusion
  139.2 2.7 constant_dynamic-slice_fusion.2
  141.9 27.1 %collective-permute-done.2 = f32[1536,256]{1,0:T(8,128)} collective-permute-done((f32[1536,256]{1,0:T(8,128)S(1)}, f32[1536,256]{1,0:T(8,128)}, u32[]{:S(2)}, u32[]{:S(2)}) %collective-permute-start.2) | collective-permute-done | bytes 1572896 | tf_op jit(solution)/shard_map/ppermute | solution.py:31
  169.3 37.4 %all-reduce.5.cloned.1.call-done = f32[256,1536]{1,0:T(8,128)} async-done(((f32[256,1536]{1,0:T(8,128)}), f32[256,1536]{1,0:T(8,128)}) %all-reduce.5.cloned.1.call-update) | async-done | bytes 1572880 | tf_op jit(solution)/shard_map/psum | solution.py:277
  206.7 4.7 fusion.8
  211.4 2.9 fusion.6
  214.2 3.5 fusion.15
  221.5 1.6 broadcast_select_fusion.4
  223.1 1.5 collective-permute-start.4
  224.6 11.7 %subtract_select_fusion.3 = f32[1536,1536]{1,0:T(8,128)S(1)} fusion(f32[1536,1536]{1,0:T(8,128)} %shard_map.74, f32[1536,256]{1,0:T(8,128)S(1)} %broadcast_select_fusion.7, f32[256,1536]{1,0:T(8,128)S(1)} %copy-done.4, pred[1536]{0:T(1024)(128)(4,1)S(1)} %get-tuple-element.46, pred[1536]{0:T(1024)(128)(4,1)S(1)} %get-tuple-element.47), kind=kOutput, calls=%fused_computation.7 | convolution fusion | flops 7254835200 | bytes 22023168 | tf_op jit(solution)/shard_map/dot_general | solution.py:314
  236.9 3.7 copy-done.2
  240.6 1.3 constant_dynamic-slice_fusion.1
  242.0 17.6 %collective-permute-done.4 = f32[1536,256]{1,0:T(8,128)S(1)} collective-permute-done((f32[1536,256]{1,0:T(8,128)S(1)}, f32[1536,256]{1,0:T(8,128)S(1)}, u32[]{:S(2)}, u32[]{:S(2)}) %collective-permute-start.4) | collective-permute-done | bytes 1572896 | tf_op jit(solution)/shard_map/ppermute | solution.py:31
  259.8 29.2 %all-reduce.7.cloned.1.call-done = f32[256,1536]{1,0:T(8,128)} async-done(((f32[256,1536]{1,0:T(8,128)}), f32[256,1536]{1,0:T(8,128)}) %all-reduce.7.cloned.1.call-update) | async-done | bytes 1572880 | tf_op jit(solution)/shard_map/psum | solution.py:277
  289.0 4.7 fusion.5
  293.7 2.9 fusion.3
  296.6 3.5 fusion.13
  302.3 1.5 collective-permute-done.5
  303.8 1.6 broadcast_select_fusion.2
  305.5 1.5 collective-permute-start.6
  307.0 11.6 %subtract_select_fusion.2 = f32[1536,1536]{1,0:T(8,128)S(1)} fusion(f32[1536,1536]{1,0:T(8,128)} %copy-done.2, f32[1536,256]{1,0:T(8,128)S(1)} %broadcast_select_fusion.5, f32[256,1536]{1,0:T(8,128)S(1)} %copy-done.5, pred[1536]{0:T(1024)(128)(4,1)S(1)} %get-tuple-element.24, pred[1536]{0:T(1024)(128)(4,1)S(1)} %get-tuple-element.23), kind=kOutput, calls=%fused_computation.6 | convolution fusion | flops 7254835200 | bytes 22023168 | tf_op jit(solution)/shard_map/dot_general | solution.py:314
  319.1 3.7 copy-done.3
  323.0 19.0 %collective-permute-done.6 = f32[1536,256]{1,0:T(8,128)S(1)} collective-permute-done((f32[1536,256]{1,0:T(8,128)S(1)}, f32[1536,256]{1,0:T(8,128)S(1)}, u32[]{:S(2)}, u32[]{:S(2)}) %collective-permute-start.6) | collective-permute-done | bytes 1572896 | tf_op jit(solution)/shard_map/ppermute | solution.py:31
  342.2 28.3 %all-reduce.9.cloned.1.call-done = f32[256,1536]{1,0:T(8,128)} async-done(((f32[256,1536]{1,0:T(8,128)}), f32[256,1536]{1,0:T(8,128)}) %all-reduce.9.cloned.1.call-update) | async-done | bytes 1572880 | tf_op jit(solution)/shard_map/psum | solution.py:277
  370.5 4.6 fusion.2
  375.1 2.4 fusion
  377.5 2.4 fusion.11
  381.0 2.5 collective-permute-done.7
  383.5 1.7 broadcast_select_fusion
  385.3 1.4 collective-permute-start.8
  386.8 13.4 %subtract_select_fusion.1 = f32[1536,1536]{1,0:T(8,128)} fusion(f32[1536,1536]{1,0:T(8,128)} %copy-done.3, f32[1536,256]{1,0:T(8,128)S(1)} %broadcast_select_fusion.3, f32[256,1536]{1,0:T(8,128)} %all-reduce.9.cloned.1.call-done, pred[1536]{0:T(1024)(128)(4,1)S(1)} %get-tuple-element.22, pred[1536]{0:T(1024)(128)(4,1)S(1)} %get-tuple-element.21), kind=kOutput, calls=%fused_computation.5 | convolution fusion | flops 7254835200 | bytes 22023168 | tf_op jit(solution)/shard_map/dot_general | solution.py:314
  400.3 2.9 select_dynamic-update-slice_fusion
  403.2 45.3 %all-reduce.11.cloned.1.call-done = f32[256,1536]{1,0:T(8,128)} async-done(((f32[256,1536]{1,0:T(8,128)}), f32[256,1536]{1,0:T(8,128)}) %all-reduce.11.cloned.1.call-update) | async-done | bytes 1572880 | tf_op jit(solution)/shard_map/psum | solution.py:277
  448.5 12.3 %subtract_select_fusion = f32[1536,1536]{1,0:T(8,128)S(1)} fusion(f32[1536,1536]{1,0:T(8,128)} %select_dynamic-update-slice_fusion, f32[256,1536]{1,0:T(8,128)} %all-reduce.11.cloned.1.call-done, pred[1536]{0:T(1024)(128)(4,1)S(1)} %get-tuple-element.20, pred[1536]{0:T(1024)(128)(4,1)S(1)} %get-tuple-element.19, f32[1536,256]{1,0:T(8,128)} %collective-permute-done.8, ...), kind=kOutput, calls=%fused_computation.4 | convolution fusion | flops 7255228416 | bytes 23596032 | tf_op jit(solution)/shard_map/dot_general | solution.py:314
  460.8 3.7 copy.81
  464.6 2.9 bitcast_dynamic-update-slice_fusion
  (131 shorter events, 15.6 us)
Async XLA Ops:
  6.5 20.9 %copy-start = (f32[1,6144]{1,0:T(1,128)S(1)}, f32[1,6144]{1,0:T(1,128)}, u32[]{:S(2)}) copy-start(f32[1,6144]{1,0:T(1,128)} %param.11) | copy-start | bytes 73732
  16.6 7.3 %copy-start.9 = (s32[1,2,16]{2,1,0:T(2,128)S(1)}, s32[1,2,16]{2,1,0:T(2,128)}, u32[]{:S(2)}) copy-start(s32[1,2,16]{2,1,0:T(2,128)} %param.8) | copy-start | bytes 388
  16.6 7.4 %copy-start.10 = (s32[1,2,16]{2,1,0:T(2,128)S(1)}, s32[1,2,16]{2,1,0:T(2,128)}, u32[]{:S(2)}) copy-start(s32[1,2,16]{2,1,0:T(2,128)} %param.9) | copy-start | bytes 388
  16.6 7.5 %copy-start.8 = (s32[1,2]{1,0:T(1,128)S(1)}, s32[1,2]{1,0:T(1,128)}, u32[]{:S(2)}) copy-start(s32[1,2]{1,0:T(1,128)} %param.10) | copy-start | bytes 28
  16.6 9.2 %copy-start.7 = (s32[1,4]{1,0:T(1,128)S(1)}, s32[1,4]{1,0:T(1,128)}, u32[]{:S(2)}) copy-start(s32[1,4]{1,0:T(1,128)} %param.12) | copy-start | bytes 52
  16.6 97.7 %all-to-all-start = ((f32[32,2,128,128]{3,2,1,0:T(8,128)}), f32[32,2,128,128]{3,2,1,0:T(8,128)}, u32[]{:S(2)}, u32[]{:S(2)}) async-start(f32[32,2,128,128]{3,2,1,0:T(8,128)} %bitcast.147), calls=%async_computation | async-start | bytes 8388608 | tf_op jit(solution)/shard_map/all_to_all | solution.py:230
  23.8 182.9 %all-reduce.5.cloned.1.call-start = ((), (), s32[]{:S(2)}) async-start(), calls=%async_computation.1 | async-start | bytes 3145728 | tf_op jit(solution)/shard_map/psum | solution.py:277
  24.1 20.0 %collective-permute-start = (s32[66]{0:T(128)S(1)}, s32[66]{0:T(128)S(1)}, u32[]{:S(2)}, u32[]{:S(2)}) collective-permute-start(s32[66]{0:T(128)S(1)} %pad_add_fusion.2), channel_id=1, source_target_pairs={{0,16},{16,0},{1,17},{17,1},{2,18},{18,2},{3,19},{19,3},{4,20},{20... | collective-permute-start | bytes 800 | tf_op jit(solution)/shard_map/ppermute | solution.py:151
  127.2 4.9 %collective-permute-start.1 = (f32[1536,256]{1,0:T(8,128)S(1)}, f32[1536,256]{1,0:T(8,128)}, u32[]{:S(2)}, u32[]{:S(2)}) collective-permute-start(f32[1536,256]{1,0:T(8,128)S(1)} %fusion.9), channel_id=1, source_target_pairs={{0,4},{4,0},{8,12},{12,8},{1,5},{5,1},{9,13},{13,9},{2,6},{6,2},{1... | collective-permute-start | bytes 4718600 | tf_op jit(solution)/shard_map/ppermute | solution.py:31
  132.3 36.7 %collective-permute-start.2 = (f32[1536,256]{1,0:T(8,128)S(1)}, f32[1536,256]{1,0:T(8,128)}, u32[]{:S(2)}, u32[]{:S(2)}) collective-permute-start(f32[1536,256]{1,0:T(8,128)S(1)} %broadcast_select_fusion.6), channel_id=1, source_target_pairs={{0,8},{4,12},{8,0},{12,4},{1,9},{5,13},{9,1},{13,5},{2,10},{6,14},... | collective-permute-start | bytes 4718600 | tf_op jit(solution)/shard_map/ppermute | solution.py:31
  136.5 152.5 %all-reduce.7.cloned.1.call-start = ((), (), s32[]{:S(2)}) async-start(), calls=%async_computation.2 | async-start | bytes 3145728 | tf_op jit(solution)/shard_map/psum | solution.py:277
  206.7 4.7 copy-start.4
  217.7 3.8 collective-permute-start.3
  220.6 150.0 %all-reduce.9.cloned.1.call-start = ((), (), s32[]{:S(2)}) async-start(), calls=%async_computation.3 | async-start | bytes 3145728 | tf_op jit(solution)/shard_map/psum | solution.py:277
  223.1 36.5 %collective-permute-start.4 = (f32[1536,256]{1,0:T(8,128)S(1)}, f32[1536,256]{1,0:T(8,128)S(1)}, u32[]{:S(2)}, u32[]{:S(2)}) collective-permute-start(f32[1536,256]{1,0:T(8,128)S(1)} %broadcast_select_fusion.4), channel_id=1, source_target_pairs={{0,8},{4,12},{8,0},{12,4},{1,9},{5,13},{9,1},{13,5},{2,10},{6,14},... | collective-permute-start | bytes 4718600 | tf_op jit(solution)/shard_map/ppermute | solution.py:31
  236.9 3.7 copy-start.2
  289.0 4.7 copy-start.5
  300.1 3.8 collective-permute-start.5
  302.0 146.4 %all-reduce.11.cloned.1.call-start = ((), (), s32[]{:S(2)}) async-start(), calls=%async_computation.4 | async-start | bytes 3145728 | tf_op jit(solution)/shard_map/psum | solution.py:277
  305.5 36.5 %collective-permute-start.6 = (f32[1536,256]{1,0:T(8,128)S(1)}, f32[1536,256]{1,0:T(8,128)S(1)}, u32[]{:S(2)}, u32[]{:S(2)}) collective-permute-start(f32[1536,256]{1,0:T(8,128)S(1)} %broadcast_select_fusion.2), channel_id=1, source_target_pairs={{0,8},{4,12},{8,0},{12,4},{1,9},{5,13},{9,1},{13,5},{2,10},{6,14},... | collective-permute-start | bytes 4718600 | tf_op jit(solution)/shard_map/ppermute | solution.py:31
  319.1 3.7 copy-start.3
  379.9 1.1 copy-start.6
  379.9 3.6 collective-permute-start.7
  385.3 63.2 %collective-permute-start.8 = (f32[1536,256]{1,0:T(8,128)S(1)}, f32[1536,256]{1,0:T(8,128)}, u32[]{:S(2)}, u32[]{:S(2)}) collective-permute-start(f32[1536,256]{1,0:T(8,128)S(1)} %broadcast_select_fusion), channel_id=1, source_target_pairs={{0,8},{4,12},{8,0},{12,4},{1,9},{5,13},{9,1},{13,5},{2,10},{6,14},... | collective-permute-start | bytes 4718600 | tf_op jit(solution)/shard_map/ppermute | solution.py:31
  464.6 2.9 copy-start.1
Sparse Core Ops, SparseCore 0:
  136.6 69.9 all-reduce.4
  220.7 68.3 all-reduce.6
  302.2 68.3 all-reduce.8
  380.2 68.2 all-reduce.10

commit v4 on v0

--- a/solution.py
+++ b/solution.py
@@ -93,13 +93,25 @@
     row_tiles = rows_total // tile_side
     col_tiles = cols_total // tile_side
     offset = offset_ref[0]
-    for band in range(row_tiles):
-        band_rows = pl.ds(band * tile_side, tile_side)
-        row_iota = lax.broadcasted_iota(jnp.int32, (tile_side, cols_total), 0) + band * tile_side
-        col_iota = lax.broadcasted_iota(jnp.int32, (tile_side, cols_total), 1)
-        out_ref[band_rows, :] = jnp.where(
-            row_iota + offset == col_iota, diag_ref[band_rows, :], 0.0
-        )
+    if rows_total == cols_total:
+        out_ref[...] = jnp.zeros(out_ref.shape, out_ref.dtype)
+        row_iota = lax.broadcasted_iota(jnp.int32, (tile_side, tile_side), 0)
+        col_iota = lax.broadcasted_iota(jnp.int32, (tile_side, tile_side), 1)
+
+        @pl.when(offset == 0)
+        def _():
+            for band in range(row_tiles):
+                span = pl.ds(band * tile_side, tile_side)
+                out_ref[span, span] = jnp.where(row_iota == col_iota, diag_ref[span, :], 0.0)
+
+    else:
+        for band in range(row_tiles):
+            band_rows = pl.ds(band * tile_side, tile_side)
+            row_iota = lax.broadcasted_iota(jnp.int32, (tile_side, cols_total), 0) + band * tile_side
+            col_iota = lax.broadcasted_iota(jnp.int32, (tile_side, cols_total), 1)
+            out_ref[band_rows, :] = jnp.where(
+                row_iota + offset == col_iota, diag_ref[band_rows, :], 0.0
+            )
 
     def add_tile(slot, carry):
         spot = spots_ref[slot]

time: 482 us -> 481 us (level)
  transfers between devices with their start and end apart: 13 -> 13, of which waited for: 12 -> 12; matrix products, arithmetic and copies ran while one was open for 14% -> 13% of each run, Pallas kernels for 0% -> 0%
where the time goes in v4:
time: 481 us; the launch traced here: 472 us
  waiting for transfers between devices  273 us (57%)
  matrix products  82.9 us (17%)
  local copies, waits for them, and re-layouts  25 us (5%)
  between operations  22.4 us (5%)
  other arithmetic  20.3 us (4%)
  blocking collectives  17.4 us (4%)
  Pallas kernels  15.7 us (3%)
  starting transfers between devices  15.3 us (3%)
    psum x4, waiting for transfers between devices, share_strips(): top_strip = lax.psum(row_strip, 'row')  140 us
    ppermute x8, waiting for transfers between devices, exchange_broadcast(): received = lax.ppermute(block, axis, partner)  69.1 us
    all_to_all x1, waiting for transfers between devices, body(): lax.all_to_all(payload, ('front', 'column', 'row'), split_axis=0, concat_...  63.8 us
    dot_general x4, matrix products, body(): jnp.dot(left_strip, top_strip, precision=HIGHEST, preferred_element_type=...  48.6 us
    unnamed x1, blocking collectives  17.4 us
    dot_general x3, matrix products, body(): jnp.dot(left_part, top_strip, precision=HIGHEST, preferred_element_type=j...  14 us
    unnamed x27, local copies, waits for them, and re-layouts  12.8 us
    dot_general x4, matrix products, share_strips(): jnp.dot(col_strip, inverses[step_index], precision=HIGHEST, preferred_ele...  12.3 us
  transfers between devices with their start and end apart: 13, of which 12 were waited for; matrix products, arithmetic and copies ran while one was open for 13% of the time, Pallas kernels for 0%

profile of v4, /device:TPU:0, one launch (start us, length us, event | category | flops | bytes accessed | tf_op | source)
XLA Modules:
  0.0 472.3 jit_solution(7669762554371651689)
XLA Ops:
  9.2 1.2 scatter_custom_fusion.sources_ref
  10.4 6.2 %shard_map.73 = f32[64,128,128]{2,1,0:T(8,128)} custom-call(s32[64]{0:T(128)} %scatter_custom_fusion.sources_ref, f32[1,2,512,512]{3,2,1,0:T(8,128)} %blocks_ref.1), custom_call_target="tpu_custom_call" | custom-call | tf_op jit(solution)/shard_map/pallas_call | solution.py:77
  16.6 7.1 %all-to-all-start = ((f32[32,2,128,128]{3,2,1,0:T(8,128)}), f32[32,2,128,128]{3,2,1,0:T(8,128)}, u32[]{:S(2)}, u32[]{:S(2)}) async-start(f32[32,2,128,128]{3,2,1,0:T(8,128)} %bitcast.143), calls=%async_computation | async-start | bytes 8388608 | tf_op jit(solution)/shard_map/all_to_all | solution.py:236
  26.7 17.4 %all-reduce = s32[132]{0:T(256)S(1)} all-reduce(s32[132]{0:T(256)S(1)} %add_dynamic-update-slice_fusion), channel_id=2, replica_groups=mesh['front'=2,'column'=4,'row'=4] {'front'}, use_global_device_ids=true, to_apply=%add | all-reduce | flops 132 | bytes 1056
  49.3 1.2 copy.73.diag_ref
  50.5 63.8 %all-to-all-done = f32[32,2,128,128]{3,2,1,0:T(8,128)} async-done(((f32[32,2,128,128]{3,2,1,0:T(8,128)}), f32[32,2,128,128]{3,2,1,0:T(8,128)}, u32[]{:S(2)}, u32[]{:S(2)}) %all-to-all-start) | async-done | bytes 4194336 | tf_op jit(solution)/shard_map/all_to_all | solution.py:236
  114.2 9.5 %shard_map.74 = f32[1536,1536]{1,0:T(8,128)} custom-call(s32[64]{0:T(128)} %reshape.602.spots_ref, s32[1]{0:T(128)} %bitcast.16.offset_ref, f32[1536,1]{1,0:T(8,128)} %copy.73.diag_ref, f32[64,128,128]{2,1,0:T(8,128)} %bitcast.25.payload_ref), custom_call_target="tpu_custom_call" | custom-call | tf_op jit(solution)/shard_map/pallas_call | solution.py:137
  123.8 2.9 fusion.9
  126.7 1.5 collective-permute-start
  129.6 1.9 collective-permute-done
  131.4 1.7 broadcast_select_fusion.6
  133.1 1.5 collective-permute-start.1
  134.6 2.6 dynamic-slice_select_fusion
  139.9 2.7 constant_dynamic-slice_fusion.2
  142.6 25.9 %collective-permute-done.1 = f32[1536,256]{1,0:T(8,128)} collective-permute-done((f32[1536,256]{1,0:T(8,128)S(1)}, f32[1536,256]{1,0:T(8,128)}, u32[]{:S(2)}, u32[]{:S(2)}) %collective-permute-start.1) | collective-permute-done | bytes 1572896 | tf_op jit(solution)/shard_map/ppermute | solution.py:31
  168.9 37.6 %all-reduce.6.cloned.1.call-done = f32[256,1536]{1,0:T(8,128)} async-done(((f32[256,1536]{1,0:T(8,128)}), f32[256,1536]{1,0:T(8,128)}) %all-reduce.6.cloned.1.call-update) | async-done | bytes 1572880 | tf_op jit(solution)/shard_map/psum | solution.py:283
  206.4 4.7 fusion.8
  211.1 2.9 fusion.6
  214.0 3.5 fusion.15
  221.2 1.6 broadcast_select_fusion.4
  222.9 1.5 collective-permute-start.3
  224.4 11.7 %subtract_select_fusion.3 = f32[1536,1536]{1,0:T(8,128)S(1)} fusion(f32[1536,1536]{1,0:T(8,128)} %shard_map.74, f32[1536,256]{1,0:T(8,128)S(1)} %broadcast_select_fusion.7, f32[256,1536]{1,0:T(8,128)S(1)} %copy-done.4, pred[1536]{0:T(1024)(128)(4,1)S(1)} %get-tuple-element.46, pred[1536]{0:T(1024)(128)(4,1)S(1)} %get-tuple-element.47), kind=kOutput, calls=%fused_computation.6 | convolution fusion | flops 7254835200 | bytes 22023168 | tf_op jit(solution)/shard_map/dot_general | solution.py:320
  236.6 3.7 copy-done.2
  240.4 1.3 constant_dynamic-slice_fusion.1
  241.7 17.7 %collective-permute-done.3 = f32[1536,256]{1,0:T(8,128)S(1)} collective-permute-done((f32[1536,256]{1,0:T(8,128)S(1)}, f32[1536,256]{1,0:T(8,128)S(1)}, u32[]{:S(2)}, u32[]{:S(2)}) %collective-permute-start.3) | collective-permute-done | bytes 1572896 | tf_op jit(solution)/shard_map/ppermute | solution.py:31
  259.6 29.2 %all-reduce.8.cloned.1.call-done = f32[256,1536]{1,0:T(8,128)} async-done(((f32[256,1536]{1,0:T(8,128)}), f32[256,1536]{1,0:T(8,128)}) %all-reduce.8.cloned.1.call-update) | async-done | bytes 1572880 | tf_op jit(solution)/shard_map/psum | solution.py:283
  288.8 4.7 fusion.5
  293.5 2.9 fusion.3
  296.4 3.5 fusion.13
  302.1 1.5 collective-permute-done.4
  303.6 1.6 broadcast_select_fusion.2
  305.2 1.5 collective-permute-start.5
  306.8 11.6 %subtract_select_fusion.2 = f32[1536,1536]{1,0:T(8,128)S(1)} fusion(f32[1536,1536]{1,0:T(8,128)} %copy-done.2, f32[1536,256]{1,0:T(8,128)S(1)} %broadcast_select_fusion.5, f32[256,1536]{1,0:T(8,128)S(1)} %copy-done.5, pred[1536]{0:T(1024)(128)(4,1)S(1)} %get-tuple-element.24, pred[1536]{0:T(1024)(128)(4,1)S(1)} %get-tuple-element.23), kind=kOutput, calls=%fused_computation.5 | convolution fusion | flops 7254835200 | bytes 22023168 | tf_op jit(solution)/shard_map/dot_general | solution.py:320
  318.8 3.7 copy-done.3
  322.8 19.0 %collective-permute-done.5 = f32[1536,256]{1,0:T(8,128)S(1)} collective-permute-done((f32[1536,256]{1,0:T(8,128)S(1)}, f32[1536,256]{1,0:T(8,128)S(1)}, u32[]{:S(2)}, u32[]{:S(2)}) %collective-permute-start.5) | collective-permute-done | bytes 1572896 | tf_op jit(solution)/shard_map/ppermute | solution.py:31
  341.9 28.3 %all-reduce.10.cloned.1.call-done = f32[256,1536]{1,0:T(8,128)} async-done(((f32[256,1536]{1,0:T(8,128)}), f32[256,1536]{1,0:T(8,128)}) %all-reduce.10.cloned.1.call-update) | async-done | bytes 1572880 | tf_op jit(solution)/shard_map/psum | solution.py:283
  370.3 4.6 fusion.2
  374.8 2.4 fusion
  377.3 2.4 fusion.11
  380.8 2.5 collective-permute-done.6
  383.3 1.7 broadcast_select_fusion
  385.0 1.4 collective-permute-start.7
  386.6 13.4 %subtract_select_fusion.1 = f32[1536,1536]{1,0:T(8,128)} fusion(f32[1536,1536]{1,0:T(8,128)} %copy-done.3, f32[1536,256]{1,0:T(8,128)S(1)} %broadcast_select_fusion.3, f32[256,1536]{1,0:T(8,128)} %all-reduce.10.cloned.1.call-done, pred[1536]{0:T(1024)(128)(4,1)S(1)} %get-tuple-element.22, pred[1536]{0:T(1024)(128)(4,1)S(1)} %get-tuple-element.21), kind=kOutput, calls=%fused_computation.4 | convolution fusion | flops 7254835200 | bytes 22023168 | tf_op jit(solution)/shard_map/dot_general | solution.py:320
  400.0 2.9 select_dynamic-update-slice_fusion
  402.9 45.3 %all-reduce.12.cloned.1.call-done = f32[256,1536]{1,0:T(8,128)} async-done(((f32[256,1536]{1,0:T(8,128)}), f32[256,1536]{1,0:T(8,128)}) %all-reduce.12.cloned.1.call-update) | async-done | bytes 1572880 | tf_op jit(solution)/shard_map/psum | solution.py:283
  448.2 11.8 %subtract_select_fusion = f32[1536,1536]{1,0:T(8,128)S(1)} fusion(f32[1536,1536]{1,0:T(8,128)} %select_dynamic-update-slice_fusion, f32[256,1536]{1,0:T(8,128)} %all-reduce.12.cloned.1.call-done, pred[1536]{0:T(1024)(128)(4,1)S(1)} %get-tuple-element.20, pred[1536]{0:T(1024)(128)(4,1)S(1)} %get-tuple-element.19, f32[1536,256]{1,0:T(8,128)} %collective-permute-done.7, ...), kind=kOutput, calls=%fused_computation.3 | convolution fusion | flops 7255228416 | bytes 23596032 | tf_op jit(solution)/shard_map/dot_general | solution.py:320
  460.1 3.7 copy.82
  463.8 1.5 bitcast_dynamic-update-slice_fusion
  (128 shorter events, 15.3 us)
Async XLA Ops:
  6.5 42.7 %copy-start = (f32[1,6144]{1,0:T(1,128)S(1)}, f32[1,6144]{1,0:T(1,128)}, u32[]{:S(2)}) copy-start(f32[1,6144]{1,0:T(1,128)} %param.11) | copy-start | bytes 73732
  16.6 7.2 %copy-start.9 = (s32[1,2,16]{2,1,0:T(2,128)S(1)}, s32[1,2,16]{2,1,0:T(2,128)}, u32[]{:S(2)}) copy-start(s32[1,2,16]{2,1,0:T(2,128)} %param.8) | copy-start | bytes 388
  16.6 7.3 %copy-start.10 = (s32[1,2,16]{2,1,0:T(2,128)S(1)}, s32[1,2,16]{2,1,0:T(2,128)}, u32[]{:S(2)}) copy-start(s32[1,2,16]{2,1,0:T(2,128)} %param.9) | copy-start | bytes 388
  16.6 7.4 %copy-start.7 = (s32[1,4]{1,0:T(1,128)S(1)}, s32[1,4]{1,0:T(1,128)}, u32[]{:S(2)}) copy-start(s32[1,4]{1,0:T(1,128)} %param.12) | copy-start | bytes 52
  16.6 8.7 %copy-start.11 = (u32[32]{0:T(128)S(1)}, u32[32]{0:T(128)}, u32[]{:S(2)}) copy-start(u32[32]{0:T(128)} %constant.349) | copy-start | bytes 388
  16.6 9.9 %copy-start.8 = (s32[1,2]{1,0:T(1,128)S(1)}, s32[1,2]{1,0:T(1,128)}, u32[]{:S(2)}) copy-start(s32[1,2]{1,0:T(1,128)} %param.10) | copy-start | bytes 28
  16.6 97.6 %all-to-all-start = ((f32[32,2,128,128]{3,2,1,0:T(8,128)}), f32[32,2,128,128]{3,2,1,0:T(8,128)}, u32[]{:S(2)}, u32[]{:S(2)}) async-start(f32[32,2,128,128]{3,2,1,0:T(8,128)} %bitcast.143), calls=%async_computation | async-start | bytes 8388608 | tf_op jit(solution)/shard_map/all_to_all | solution.py:236
  23.7 182.7 %all-reduce.6.cloned.1.call-start = ((), (), s32[]{:S(2)}) async-start(), calls=%async_computation.1 | async-start | bytes 3145728 | tf_op jit(solution)/shard_map/psum | solution.py:283
  126.7 4.7 collective-permute-start
  133.1 35.4 %collective-permute-start.1 = (f32[1536,256]{1,0:T(8,128)S(1)}, f32[1536,256]{1,0:T(8,128)}, u32[]{:S(2)}, u32[]{:S(2)}) collective-permute-start(f32[1536,256]{1,0:T(8,128)S(1)} %broadcast_select_fusion.6), channel_id=1, source_target_pairs={{0,8},{4,12},{8,0},{12,4},{1,9},{5,13},{9,1},{13,5},{2,10},{6,14},... | collective-permute-start | bytes 4718600 | tf_op jit(solution)/shard_map/ppermute | solution.py:31
  137.3 151.5 %all-reduce.8.cloned.1.call-start = ((), (), s32[]{:S(2)}) async-start(), calls=%async_computation.2 | async-start | bytes 3145728 | tf_op jit(solution)/shard_map/psum | solution.py:283
  206.4 4.7 copy-start.4
  217.5 3.8 collective-permute-start.2
  220.3 150.0 %all-reduce.10.cloned.1.call-start = ((), (), s32[]{:S(2)}) async-start(), calls=%async_computation.3 | async-start | bytes 3145728 | tf_op jit(solution)/shard_map/psum | solution.py:283
  222.9 36.5 %collective-permute-start.3 = (f32[1536,256]{1,0:T(8,128)S(1)}, f32[1536,256]{1,0:T(8,128)S(1)}, u32[]{:S(2)}, u32[]{:S(2)}) collective-permute-start(f32[1536,256]{1,0:T(8,128)S(1)} %broadcast_select_fusion.4), channel_id=1, source_target_pairs={{0,8},{4,12},{8,0},{12,4},{1,9},{5,13},{9,1},{13,5},{2,10},{6,14},... | collective-permute-start | bytes 4718600 | tf_op jit(solution)/shard_map/ppermute | solution.py:31
  236.6 3.7 copy-start.2
  288.8 4.7 copy-start.5
  299.8 3.8 collective-permute-start.4
  301.8 146.4 %all-reduce.12.cloned.1.call-start = ((), (), s32[]{:S(2)}) async-start(), calls=%async_computation.4 | async-start | bytes 3145728 | tf_op jit(solution)/shard_map/psum | solution.py:283
  305.2 36.5 %collective-permute-start.5 = (f32[1536,256]{1,0:T(8,128)S(1)}, f32[1536,256]{1,0:T(8,128)S(1)}, u32[]{:S(2)}, u32[]{:S(2)}) collective-permute-start(f32[1536,256]{1,0:T(8,128)S(1)} %broadcast_select_fusion.2), channel_id=1, source_target_pairs={{0,8},{4,12},{8,0},{12,4},{1,9},{5,13},{9,1},{13,5},{2,10},{6,14},... | collective-permute-start | bytes 4718600 | tf_op jit(solution)/shard_map/ppermute | solution.py:31
  318.8 3.7 copy-start.3
  379.6 1.1 copy-start.6
  379.7 3.6 collective-permute-start.6
  385.0 63.2 %collective-permute-start.7 = (f32[1536,256]{1,0:T(8,128)S(1)}, f32[1536,256]{1,0:T(8,128)}, u32[]{:S(2)}, u32[]{:S(2)}) collective-permute-start(f32[1536,256]{1,0:T(8,128)S(1)} %broadcast_select_fusion), channel_id=1, source_target_pairs={{0,8},{4,12},{8,0},{12,4},{1,9},{5,13},{9,1},{13,5},{2,10},{6,14},... | collective-permute-start | bytes 4718600 | tf_op jit(solution)/shard_map/ppermute | solution.py:31
  463.8 1.5 copy-start.1
Sparse Core Ops, SparseCore 0:
  137.4 68.9 all-reduce.5
  220.4 68.3 all-reduce.7
  301.9 68.3 all-reduce.9
  379.9 68.2 all-reduce.11

commit v5 on v4

--- a/solution.py
+++ b/solution.py
@@ -52,10 +52,6 @@
             out_ref[slot] = blocks_ref[
                 0, child, pl.ds(row_start, tile_side), pl.ds(col_start, tile_side)
             ]
-
-        @pl.when(source < 0)
-        def _():
-            out_ref[slot] = jnp.zeros((tile_side, tile_side), out_ref.dtype)
 
         return carry
 

time: 481 us -> 481 us (level)
  transfers between devices with their start and end apart: 13 -> 13, of which waited for: 12 -> 12; matrix products, arithmetic and copies ran while one was open for 13% -> 14% of each run, Pallas kernels for 0% -> 0%
where the time goes in v5:
time: 481 us; the launch traced here: 473 us
  waiting for transfers between devices  273 us (57%)
  matrix products  83.3 us (17%)
  local copies, waits for them, and re-layouts  25 us (5%)
  between operations  22.4 us (5%)
  other arithmetic  21.7 us (5%)
  blocking collectives  17.4 us (4%)
  starting transfers between devices  15.5 us (3%)
  Pallas kernels  15.4 us (3%)
    psum x4, waiting for transfers between devices, share_strips(): top_strip = lax.psum(row_strip, 'row')  139 us
    ppermute x8, waiting for transfers between devices, exchange_broadcast(): received = lax.ppermute(block, axis, partner)  70.3 us
    all_to_all x1, waiting for transfers between devices, body(): lax.all_to_all(payload, ('front', 'column', 'row'), split_axis=0, concat_...  63.8 us
    dot_general x4, matrix products, body(): jnp.dot(left_strip, top_strip, precision=HIGHEST, preferred_element_type=...  49 us
    unnamed x1, blocking collectives  17.4 us
    dot_general x3, matrix products, body(): jnp.dot(left_part, top_strip, precision=HIGHEST, preferred_element_type=j...  14 us
    unnamed x27, local copies, waits for them, and re-layouts  12.8 us
    dot_general x4, matrix products, share_strips(): jnp.dot(col_strip, inverses[step_index], precision=HIGHEST, preferred_ele...  12.2 us
  transfers between devices with their start and end apart: 13, of which 12 were waited for; matrix products, arithmetic and copies ran while one was open for 14% of the time, Pallas kernels for 0%

profile of v5, /device:TPU:0, one launch (start us, length us, event | category | flops | bytes accessed | tf_op | source)
XLA Modules:
  0.0 473.5 jit_solution(15541468922559960297)
XLA Ops:
  9.2 1.2 scatter_custom_fusion.sources_ref
  10.4 5.7 %shard_map.73 = f32[64,128,128]{2,1,0:T(8,128)} custom-call(s32[64]{0:T(128)} %scatter_custom_fusion.sources_ref, f32[1,2,512,512]{3,2,1,0:T(8,128)} %blocks_ref.1), custom_call_target="tpu_custom_call" | custom-call | tf_op jit(solution)/shard_map/pallas_call | solution.py:73
  16.2 7.3 %all-to-all-start = ((f32[32,2,128,128]{3,2,1,0:T(8,128)}), f32[32,2,128,128]{3,2,1,0:T(8,128)}, u32[]{:S(2)}, u32[]{:S(2)}) async-start(f32[32,2,128,128]{3,2,1,0:T(8,128)} %bitcast.143), calls=%async_computation | async-start | bytes 8388608 | tf_op jit(solution)/shard_map/all_to_all | solution.py:232
  26.5 17.4 %all-reduce = s32[132]{0:T(256)S(1)} all-reduce(s32[132]{0:T(256)S(1)} %add_dynamic-update-slice_fusion), channel_id=2, replica_groups=mesh['front'=2,'column'=4,'row'=4] {'front'}, use_global_device_ids=true, to_apply=%add | all-reduce | flops 132 | bytes 1056
  49.1 1.2 copy.73.diag_ref
  50.3 63.8 %all-to-all-done = f32[32,2,128,128]{3,2,1,0:T(8,128)} async-done(((f32[32,2,128,128]{3,2,1,0:T(8,128)}), f32[32,2,128,128]{3,2,1,0:T(8,128)}, u32[]{:S(2)}, u32[]{:S(2)}) %all-to-all-start) | async-done | bytes 4194336 | tf_op jit(solution)/shard_map/all_to_all | solution.py:232
  114.0 9.6 %shard_map.74 = f32[1536,1536]{1,0:T(8,128)} custom-call(s32[64]{0:T(128)} %reshape.602.spots_ref, s32[1]{0:T(128)} %bitcast.16.offset_ref, f32[1536,1]{1,0:T(8,128)} %copy.73.diag_ref, f32[64,128,128]{2,1,0:T(8,128)} %bitcast.25.payload_ref), custom_call_target="tpu_custom_call" | custom-call | tf_op jit(solution)/shard_map/pallas_call | solution.py:133
  123.7 2.9 fusion.9
  126.5 1.5 collective-permute-start
  129.4 1.9 collective-permute-done
  131.5 1.5 collective-permute-start.1
  133.1 2.6 dynamic-slice_select_fusion
  138.4 2.7 constant_dynamic-slice_fusion.2
  141.1 27.1 %collective-permute-done.1 = f32[1536,256]{1,0:T(8,128)} collective-permute-done((f32[1536,256]{1,0:T(8,128)S(1)}, f32[1536,256]{1,0:T(8,128)}, u32[]{:S(2)}, u32[]{:S(2)}) %collective-permute-start.1) | collective-permute-done | bytes 1572896 | tf_op jit(solution)/shard_map/ppermute | solution.py:31
  168.2 1.7 broadcast_select_fusion.7
  169.9 35.8 %all-reduce.6.cloned.1.call-done = f32[256,1536]{1,0:T(8,128)} async-done(((f32[256,1536]{1,0:T(8,128)}), f32[256,1536]{1,0:T(8,128)}) %all-reduce.6.cloned.1.call-update) | async-done | bytes 1572880 | tf_op jit(solution)/shard_map/psum | solution.py:279
  205.7 4.7 fusion.8
  210.4 2.9 fusion.6
  213.2 3.5 fusion.15
  220.5 1.6 broadcast_select_fusion.4
  222.1 1.5 collective-permute-start.3
  223.6 11.7 %subtract_select_fusion.3 = f32[1536,1536]{1,0:T(8,128)S(1)} fusion(f32[1536,1536]{1,0:T(8,128)} %shard_map.74, f32[1536,256]{1,0:T(8,128)S(1)} %broadcast_select_fusion.7, f32[256,1536]{1,0:T(8,128)S(1)} %copy-done.4, pred[1536]{0:T(1024)(128)(4,1)S(1)} %get-tuple-element.46, pred[1536]{0:T(1024)(128)(4,1)S(1)} %get-tuple-element.47), kind=kOutput, calls=%fused_computation.6 | convolution fusion | flops 7254835200 | bytes 22023168 | tf_op jit(solution)/shard_map/dot_general | solution.py:316
  235.9 3.7 copy-done.2
  239.6 1.3 constant_dynamic-slice_fusion.1
  241.0 17.7 %collective-permute-done.3 = f32[1536,256]{1,0:T(8,128)S(1)} collective-permute-done((f32[1536,256]{1,0:T(8,128)S(1)}, f32[1536,256]{1,0:T(8,128)S(1)}, u32[]{:S(2)}, u32[]{:S(2)}) %collective-permute-start.3) | collective-permute-done | bytes 1572896 | tf_op jit(solution)/shard_map/ppermute | solution.py:31
  258.8 29.2 %all-reduce.8.cloned.1.call-done = f32[256,1536]{1,0:T(8,128)} async-done(((f32[256,1536]{1,0:T(8,128)}), f32[256,1536]{1,0:T(8,128)}) %all-reduce.8.cloned.1.call-update) | async-done | bytes 1572880 | tf_op jit(solution)/shard_map/psum | solution.py:279
  288.0 4.7 fusion.5
  292.7 2.9 fusion.3
  295.6 3.5 fusion.13
  301.3 1.5 collective-permute-done.4
  302.8 1.6 broadcast_select_fusion.2
  304.4 1.5 collective-permute-start.5
  306.0 11.6 %subtract_select_fusion.2 = f32[1536,1536]{1,0:T(8,128)S(1)} fusion(f32[1536,1536]{1,0:T(8,128)} %copy-done.2, f32[1536,256]{1,0:T(8,128)S(1)} %broadcast_select_fusion.5, f32[256,1536]{1,0:T(8,128)S(1)} %copy-done.5, pred[1536]{0:T(1024)(128)(4,1)S(1)} %get-tuple-element.24, pred[1536]{0:T(1024)(128)(4,1)S(1)} %get-tuple-element.23), kind=kOutput, calls=%fused_computation.5 | convolution fusion | flops 7254835200 | bytes 22023168 | tf_op jit(solution)/shard_map/dot_general | solution.py:316
  318.1 3.7 copy-done.3
  322.0 19.0 %collective-permute-done.5 = f32[1536,256]{1,0:T(8,128)S(1)} collective-permute-done((f32[1536,256]{1,0:T(8,128)S(1)}, f32[1536,256]{1,0:T(8,128)S(1)}, u32[]{:S(2)}, u32[]{:S(2)}) %collective-permute-start.5) | collective-permute-done | bytes 1572896 | tf_op jit(solution)/shard_map/ppermute | solution.py:31
  341.1 28.3 %all-reduce.10.cloned.1.call-done = f32[256,1536]{1,0:T(8,128)} async-done(((f32[256,1536]{1,0:T(8,128)}), f32[256,1536]{1,0:T(8,128)}) %all-reduce.10.cloned.1.call-update) | async-done | bytes 1572880 | tf_op jit(solution)/shard_map/psum | solution.py:279
  369.5 4.6 fusion.2
  374.1 2.4 fusion
  376.5 2.4 fusion.11
  380.0 2.5 collective-permute-done.6
  382.5 1.7 broadcast_select_fusion
  384.2 1.4 collective-permute-start.7
  385.8 13.4 %subtract_select_fusion.1 = f32[1536,1536]{1,0:T(8,128)} fusion(f32[1536,1536]{1,0:T(8,128)} %copy-done.3, f32[1536,256]{1,0:T(8,128)S(1)} %broadcast_select_fusion.3, f32[256,1536]{1,0:T(8,128)} %all-reduce.10.cloned.1.call-done, pred[1536]{0:T(1024)(128)(4,1)S(1)} %get-tuple-element.22, pred[1536]{0:T(1024)(128)(4,1)S(1)} %get-tuple-element.21), kind=kOutput, calls=%fused_computation.4 | convolution fusion | flops 7254835200 | bytes 22023168 | tf_op jit(solution)/shard_map/dot_general | solution.py:316
  399.2 2.9 select_dynamic-update-slice_fusion
  402.2 45.3 %all-reduce.12.cloned.1.call-done = f32[256,1536]{1,0:T(8,128)} async-done(((f32[256,1536]{1,0:T(8,128)}), f32[256,1536]{1,0:T(8,128)}) %all-reduce.12.cloned.1.call-update) | async-done | bytes 1572880 | tf_op jit(solution)/shard_map/psum | solution.py:279
  447.5 12.3 %subtract_select_fusion = f32[1536,1536]{1,0:T(8,128)S(1)} fusion(f32[1536,1536]{1,0:T(8,128)} %select_dynamic-update-slice_fusion, f32[256,1536]{1,0:T(8,128)} %all-reduce.12.cloned.1.call-done, pred[1536]{0:T(1024)(128)(4,1)S(1)} %get-tuple-element.20, pred[1536]{0:T(1024)(128)(4,1)S(1)} %get-tuple-element.19, f32[1536,256]{1,0:T(8,128)} %collective-permute-done.7, ...), kind=kOutput, calls=%fused_computation.3 | convolution fusion | flops 7255228416 | bytes 23596032 | tf_op jit(solution)/shard_map/dot_general | solution.py:316
  459.8 3.7 copy.82
  463.5 3.0 bitcast_dynamic-update-slice_fusion
  (128 shorter events, 15.3 us)
Async XLA Ops:
  6.5 42.5 %copy-start = (f32[1,6144]{1,0:T(1,128)S(1)}, f32[1,6144]{1,0:T(1,128)}, u32[]{:S(2)}) copy-start(f32[1,6144]{1,0:T(1,128)} %param.11) | copy-start | bytes 73732
  16.1 7.4 %copy-start.9 = (s32[1,2,16]{2,1,0:T(2,128)S(1)}, s32[1,2,16]{2,1,0:T(2,128)}, u32[]{:S(2)}) copy-start(s32[1,2,16]{2,1,0:T(2,128)} %param.8) | copy-start | bytes 388
  16.1 7.5 %copy-start.10 = (s32[1,2,16]{2,1,0:T(2,128)S(1)}, s32[1,2,16]{2,1,0:T(2,128)}, u32[]{:S(2)}) copy-start(s32[1,2,16]{2,1,0:T(2,128)} %param.9) | copy-start | bytes 388
  16.1 7.6 %copy-start.7 = (s32[1,4]{1,0:T(1,128)S(1)}, s32[1,4]{1,0:T(1,128)}, u32[]{:S(2)}) copy-start(s32[1,4]{1,0:T(1,128)} %param.12) | copy-start | bytes 52
  16.2 8.9 %copy-start.11 = (u32[32]{0:T(128)S(1)}, u32[32]{0:T(128)}, u32[]{:S(2)}) copy-start(u32[32]{0:T(128)} %constant.349) | copy-start | bytes 388
  16.2 10.2 %copy-start.8 = (s32[1,2]{1,0:T(1,128)S(1)}, s32[1,2]{1,0:T(1,128)}, u32[]{:S(2)}) copy-start(s32[1,2]{1,0:T(1,128)} %param.10) | copy-start | bytes 28
  16.2 97.9 %all-to-all-start = ((f32[32,2,128,128]{3,2,1,0:T(8,128)}), f32[32,2,128,128]{3,2,1,0:T(8,128)}, u32[]{:S(2)}, u32[]{:S(2)}) async-start(f32[32,2,128,128]{3,2,1,0:T(8,128)} %bitcast.143), calls=%async_computation | async-start | bytes 8388608 | tf_op jit(solution)/shard_map/all_to_all | solution.py:232
  23.5 182.1 %all-reduce.6.cloned.1.call-start = ((), (), s32[]{:S(2)}) async-start(), calls=%async_computation.1 | async-start | bytes 3145728 | tf_op jit(solution)/shard_map/psum | solution.py:279
  126.5 4.7 collective-permute-start
  131.5 36.7 %collective-permute-start.1 = (f32[1536,256]{1,0:T(8,128)S(1)}, f32[1536,256]{1,0:T(8,128)}, u32[]{:S(2)}, u32[]{:S(2)}) collective-permute-start(f32[1536,256]{1,0:T(8,128)S(1)} %broadcast_select_fusion.6), channel_id=1, source_target_pairs={{0,8},{4,12},{8,0},{12,4},{1,9},{5,13},{9,1},{13,5},{2,10},{6,14},... | collective-permute-start | bytes 4718600 | tf_op jit(solution)/shard_map/ppermute | solution.py:31
  135.7 152.3 %all-reduce.8.cloned.1.call-start = ((), (), s32[]{:S(2)}) async-start(), calls=%async_computation.2 | async-start | bytes 3145728 | tf_op jit(solution)/shard_map/psum | solution.py:279
  205.7 4.7 copy-start.4
  216.7 3.8 collective-permute-start.2
  219.6 149.9 %all-reduce.10.cloned.1.call-start = ((), (), s32[]{:S(2)}) async-start(), calls=%async_computation.3 | async-start | bytes 3145728 | tf_op jit(solution)/shard_map/psum | solution.py:279
  222.1 36.5 %collective-permute-start.3 = (f32[1536,256]{1,0:T(8,128)S(1)}, f32[1536,256]{1,0:T(8,128)S(1)}, u32[]{:S(2)}, u32[]{:S(2)}) collective-permute-start(f32[1536,256]{1,0:T(8,128)S(1)} %broadcast_select_fusion.4), channel_id=1, source_target_pairs={{0,8},{4,12},{8,0},{12,4},{1,9},{5,13},{9,1},{13,5},{2,10},{6,14},... | collective-permute-start | bytes 4718600 | tf_op jit(solution)/shard_map/ppermute | solution.py:31
  235.9 3.7 copy-start.2
  288.0 4.7 copy-start.5
  299.1 3.8 collective-permute-start.4
  301.0 146.4 %all-reduce.12.cloned.1.call-start = ((), (), s32[]{:S(2)}) async-start(), calls=%async_computation.4 | async-start | bytes 3145728 | tf_op jit(solution)/shard_map/psum | solution.py:279
  304.4 36.5 %collective-permute-start.5 = (f32[1536,256]{1,0:T(8,128)S(1)}, f32[1536,256]{1,0:T(8,128)S(1)}, u32[]{:S(2)}, u32[]{:S(2)}) collective-permute-start(f32[1536,256]{1,0:T(8,128)S(1)} %broadcast_select_fusion.2), channel_id=1, source_target_pairs={{0,8},{4,12},{8,0},{12,4},{1,9},{5,13},{9,1},{13,5},{2,10},{6,14},... | collective-permute-start | bytes 4718600 | tf_op jit(solution)/shard_map/ppermute | solution.py:31
  318.1 3.7 copy-start.3
  378.9 1.1 copy-start.6
  378.9 3.6 collective-permute-start.6
  384.2 63.2 %collective-permute-start.7 = (f32[1536,256]{1,0:T(8,128)S(1)}, f32[1536,256]{1,0:T(8,128)}, u32[]{:S(2)}, u32[]{:S(2)}) collective-permute-start(f32[1536,256]{1,0:T(8,128)S(1)} %broadcast_select_fusion), channel_id=1, source_target_pairs={{0,8},{4,12},{8,0},{12,4},{1,9},{5,13},{9,1},{13,5},{2,10},{6,14},... | collective-permute-start | bytes 4718600 | tf_op jit(solution)/shard_map/ppermute | solution.py:31
  463.5 3.0 copy-start.1
Sparse Core Ops, SparseCore 0:
  135.8 69.7 all-reduce.5
  219.7 68.3 all-reduce.7
  301.1 68.3 all-reduce.9
  379.2 68.2 all-reduce.11

commit v6 on v5

--- a/solution.py
+++ b/solution.py
@@ -55,7 +55,7 @@
 
         return carry
 
-    lax.fori_loop(0, out_ref.shape[0], place, 0)
+    lax.fori_loop(0, out_ref.shape[0], place, 0, unroll=8)
 
 
 def pack_tiles(blocks, target_dev, dest_count, capacity):
@@ -123,7 +123,7 @@
 
         return carry
 
-    lax.fori_loop(0, payload_ref.shape[0], add_tile, 0)
+    lax.fori_loop(0, payload_ref.shape[0], add_tile, 0, unroll=8)
 
 
 def scatter_tiles(payload, labels, diag_part, offset, local_rows, local_cols):

time: 481 us -> 481 us (level)
  transfers between devices with their start and end apart: 13 -> 13, of which waited for: 12 -> 12; matrix products, arithmetic and copies ran while one was open for 14% -> 13% of each run, Pallas kernels for 0% -> 0%
where the time goes in v6:
time: 481 us; the launch traced here: 473 us
  waiting for transfers between devices  274 us (57%)
  matrix products  83.4 us (17%)
  local copies, waits for them, and re-layouts  25 us (5%)
  between operations  22.4 us (5%)
  other arithmetic  20.3 us (4%)
  blocking collectives  17.4 us (4%)
  starting transfers between devices  15.6 us (3%)
  Pallas kernels  14.8 us (3%)
    psum x4, waiting for transfers between devices, share_strips(): top_strip = lax.psum(row_strip, 'row')  140 us
    ppermute x8, waiting for transfers between devices, exchange_broadcast(): received = lax.ppermute(block, axis, partner)  70.3 us
    all_to_all x1, waiting for transfers between devices, body(): lax.all_to_all(payload, ('front', 'column', 'row'), split_axis=0, concat_...  63.8 us
    dot_general x4, matrix products, body(): jnp.dot(left_strip, top_strip, precision=HIGHEST, preferred_element_type=...  49 us
    unnamed x1, blocking collectives  17.4 us
    dot_general x3, matrix products, body(): jnp.dot(left_part, top_strip, precision=HIGHEST, preferred_element_type=j...  14 us
    unnamed x27, local copies, waits for them, and re-layouts  12.8 us
    dot_general x4, matrix products, share_strips(): jnp.dot(col_strip, inverses[step_index], precision=HIGHEST, preferred_ele...  12.3 us
  transfers between devices with their start and end apart: 13, of which 12 were waited for; matrix products, arithmetic and copies ran while one was open for 13% of the time, Pallas kernels for 0%

profile of v6, /device:TPU:0, one launch (start us, length us, event | category | flops | bytes accessed | tf_op | source)
XLA Modules:
  0.0 473.1 jit_solution(16561590773891691406)
XLA Ops:
  9.2 1.2 scatter_custom_fusion.sources_ref
  10.4 5.5 %shard_map.73 = f32[64,128,128]{2,1,0:T(8,128)} custom-call(s32[64]{0:T(128)} %scatter_custom_fusion.sources_ref, f32[1,2,512,512]{3,2,1,0:T(8,128)} %blocks_ref.1), custom_call_target="tpu_custom_call" | custom-call | tf_op jit(solution)/shard_map/pallas_call | solution.py:73
  15.9 7.4 %all-to-all-start = ((f32[32,2,128,128]{3,2,1,0:T(8,128)}), f32[32,2,128,128]{3,2,1,0:T(8,128)}, u32[]{:S(2)}, u32[]{:S(2)}) async-start(f32[32,2,128,128]{3,2,1,0:T(8,128)} %bitcast.143), calls=%async_computation | async-start | bytes 8388608 | tf_op jit(solution)/shard_map/all_to_all | solution.py:232
  26.3 17.4 %all-reduce = s32[132]{0:T(256)S(1)} all-reduce(s32[132]{0:T(256)S(1)} %add_dynamic-update-slice_fusion), channel_id=2, replica_groups=mesh['front'=2,'column'=4,'row'=4] {'front'}, use_global_device_ids=true, to_apply=%add | all-reduce | flops 132 | bytes 1056
  48.9 1.2 copy.73.diag_ref
  50.1 63.8 %all-to-all-done = f32[32,2,128,128]{3,2,1,0:T(8,128)} async-done(((f32[32,2,128,128]{3,2,1,0:T(8,128)}), f32[32,2,128,128]{3,2,1,0:T(8,128)}, u32[]{:S(2)}, u32[]{:S(2)}) %all-to-all-start) | async-done | bytes 4194336 | tf_op jit(solution)/shard_map/all_to_all | solution.py:232
  113.9 9.3 %shard_map.74 = f32[1536,1536]{1,0:T(8,128)} custom-call(s32[64]{0:T(128)} %reshape.602.spots_ref, s32[1]{0:T(128)} %bitcast.16.offset_ref, f32[1536,1]{1,0:T(8,128)} %copy.73.diag_ref, f32[64,128,128]{2,1,0:T(8,128)} %bitcast.25.payload_ref), custom_call_target="tpu_custom_call" | custom-call | tf_op jit(solution)/shard_map/pallas_call | solution.py:133
  123.1 2.9 fusion.9
  126.1 1.5 collective-permute-start
  128.9 1.9 collective-permute-done
  131.1 1.5 collective-permute-start.1
  132.6 2.6 dynamic-slice_select_fusion
  137.9 2.7 constant_dynamic-slice_fusion.2
  140.6 27.1 %collective-permute-done.1 = f32[1536,256]{1,0:T(8,128)} collective-permute-done((f32[1536,256]{1,0:T(8,128)S(1)}, f32[1536,256]{1,0:T(8,128)}, u32[]{:S(2)}, u32[]{:S(2)}) %collective-permute-start.1) | collective-permute-done | bytes 1572896 | tf_op jit(solution)/shard_map/ppermute | solution.py:31
  168.0 37.3 %all-reduce.6.cloned.1.call-done = f32[256,1536]{1,0:T(8,128)} async-done(((f32[256,1536]{1,0:T(8,128)}), f32[256,1536]{1,0:T(8,128)}) %all-reduce.6.cloned.1.call-update) | async-done | bytes 1572880 | tf_op jit(solution)/shard_map/psum | solution.py:279
  205.3 4.7 fusion.8
  210.0 2.9 fusion.6
  212.9 3.5 fusion.15
  220.1 1.6 broadcast_select_fusion.4
  221.7 1.5 collective-permute-start.3
  223.3 11.7 %subtract_select_fusion.3 = f32[1536,1536]{1,0:T(8,128)S(1)} fusion(f32[1536,1536]{1,0:T(8,128)} %shard_map.74, f32[1536,256]{1,0:T(8,128)S(1)} %broadcast_select_fusion.7, f32[256,1536]{1,0:T(8,128)S(1)} %copy-done.4, pred[1536]{0:T(1024)(128)(4,1)S(1)} %get-tuple-element.46, pred[1536]{0:T(1024)(128)(4,1)S(1)} %get-tuple-element.47), kind=kOutput, calls=%fused_computation.6 | convolution fusion | flops 7254835200 | bytes 22023168 | tf_op jit(solution)/shard_map/dot_general | solution.py:316
  235.5 3.7 copy-done.2
  239.3 1.3 constant_dynamic-slice_fusion.1
  240.6 17.6 %collective-permute-done.3 = f32[1536,256]{1,0:T(8,128)S(1)} collective-permute-done((f32[1536,256]{1,0:T(8,128)S(1)}, f32[1536,256]{1,0:T(8,128)S(1)}, u32[]{:S(2)}, u32[]{:S(2)}) %collective-permute-start.3) | collective-permute-done | bytes 1572896 | tf_op jit(solution)/shard_map/ppermute | solution.py:31
  258.4 29.2 %all-reduce.8.cloned.1.call-done = f32[256,1536]{1,0:T(8,128)} async-done(((f32[256,1536]{1,0:T(8,128)}), f32[256,1536]{1,0:T(8,128)}) %all-reduce.8.cloned.1.call-update) | async-done | bytes 1572880 | tf_op jit(solution)/shard_map/psum | solution.py:279
  287.7 4.7 fusion.5
  292.4 2.9 fusion.3
  295.2 3.5 fusion.13
  300.9 1.5 collective-permute-done.4
  302.5 1.6 broadcast_select_fusion.2
  304.1 1.5 collective-permute-start.5
  305.6 11.6 %subtract_select_fusion.2 = f32[1536,1536]{1,0:T(8,128)S(1)} fusion(f32[1536,1536]{1,0:T(8,128)} %copy-done.2, f32[1536,256]{1,0:T(8,128)S(1)} %broadcast_select_fusion.5, f32[256,1536]{1,0:T(8,128)S(1)} %copy-done.5, pred[1536]{0:T(1024)(128)(4,1)S(1)} %get-tuple-element.24, pred[1536]{0:T(1024)(128)(4,1)S(1)} %get-tuple-element.23), kind=kOutput, calls=%fused_computation.5 | convolution fusion | flops 7254835200 | bytes 22023168 | tf_op jit(solution)/shard_map/dot_general | solution.py:316
  317.7 3.7 copy-done.3
  321.6 19.0 %collective-permute-done.5 = f32[1536,256]{1,0:T(8,128)S(1)} collective-permute-done((f32[1536,256]{1,0:T(8,128)S(1)}, f32[1536,256]{1,0:T(8,128)S(1)}, u32[]{:S(2)}, u32[]{:S(2)}) %collective-permute-start.5) | collective-permute-done | bytes 1572896 | tf_op jit(solution)/shard_map/ppermute | solution.py:31
  340.8 28.3 %all-reduce.10.cloned.1.call-done = f32[256,1536]{1,0:T(8,128)} async-done(((f32[256,1536]{1,0:T(8,128)}), f32[256,1536]{1,0:T(8,128)}) %all-reduce.10.cloned.1.call-update) | async-done | bytes 1572880 | tf_op jit(solution)/shard_map/psum | solution.py:279
  369.1 4.6 fusion.2
  373.7 2.4 fusion
  376.1 2.4 fusion.11
  378.7 1.0 copy-done.6
  379.7 2.5 collective-permute-done.6
  382.1 1.7 broadcast_select_fusion
  383.9 1.4 collective-permute-start.7
  385.5 13.4 %subtract_select_fusion.1 = f32[1536,1536]{1,0:T(8,128)} fusion(f32[1536,1536]{1,0:T(8,128)} %copy-done.3, f32[1536,256]{1,0:T(8,128)S(1)} %broadcast_select_fusion.3, f32[256,1536]{1,0:T(8,128)} %all-reduce.10.cloned.1.call-done, pred[1536]{0:T(1024)(128)(4,1)S(1)} %get-tuple-element.22, pred[1536]{0:T(1024)(128)(4,1)S(1)} %get-tuple-element.21), kind=kOutput, calls=%fused_computation.4 | convolution fusion | flops 7254835200 | bytes 22023168 | tf_op jit(solution)/shard_map/dot_general | solution.py:316
  398.9 2.9 select_dynamic-update-slice_fusion
  401.8 45.3 %all-reduce.12.cloned.1.call-done = f32[256,1536]{1,0:T(8,128)} async-done(((f32[256,1536]{1,0:T(8,128)}), f32[256,1536]{1,0:T(8,128)}) %all-reduce.12.cloned.1.call-update) | async-done | bytes 1572880 | tf_op jit(solution)/shard_map/psum | solution.py:279
  447.1 12.3 %subtract_select_fusion = f32[1536,1536]{1,0:T(8,128)S(1)} fusion(f32[1536,1536]{1,0:T(8,128)} %select_dynamic-update-slice_fusion, f32[256,1536]{1,0:T(8,128)} %all-reduce.12.cloned.1.call-done, pred[1536]{0:T(1024)(128)(4,1)S(1)} %get-tuple-element.20, pred[1536]{0:T(1024)(128)(4,1)S(1)} %get-tuple-element.19, f32[1536,256]{1,0:T(8,128)} %collective-permute-done.7, ...), kind=kOutput, calls=%fused_computation.3 | convolution fusion | flops 7255228416 | bytes 23596032 | tf_op jit(solution)/shard_map/dot_general | solution.py:316
  459.4 3.7 copy.82
  463.2 2.9 bitcast_dynamic-update-slice_fusion
  (128 shorter events, 14.6 us)
Async XLA Ops:
  6.5 42.4 %copy-start = (f32[1,6144]{1,0:T(1,128)S(1)}, f32[1,6144]{1,0:T(1,128)}, u32[]{:S(2)}) copy-start(f32[1,6144]{1,0:T(1,128)} %param.11) | copy-start | bytes 73732
  15.9 7.5 %copy-start.9 = (s32[1,2,16]{2,1,0:T(2,128)S(1)}, s32[1,2,16]{2,1,0:T(2,128)}, u32[]{:S(2)}) copy-start(s32[1,2,16]{2,1,0:T(2,128)} %param.8) | copy-start | bytes 388
  15.9 7.6 %copy-start.10 = (s32[1,2,16]{2,1,0:T(2,128)S(1)}, s32[1,2,16]{2,1,0:T(2,128)}, u32[]{:S(2)}) copy-start(s32[1,2,16]{2,1,0:T(2,128)} %param.9) | copy-start | bytes 388
  15.9 7.7 %copy-start.7 = (s32[1,4]{1,0:T(1,128)S(1)}, s32[1,4]{1,0:T(1,128)}, u32[]{:S(2)}) copy-start(s32[1,4]{1,0:T(1,128)} %param.12) | copy-start | bytes 52
  15.9 9.0 %copy-start.11 = (u32[32]{0:T(128)S(1)}, u32[32]{0:T(128)}, u32[]{:S(2)}) copy-start(u32[32]{0:T(128)} %constant.349) | copy-start | bytes 388
  15.9 10.2 %copy-start.8 = (s32[1,2]{1,0:T(1,128)S(1)}, s32[1,2]{1,0:T(1,128)}, u32[]{:S(2)}) copy-start(s32[1,2]{1,0:T(1,128)} %param.10) | copy-start | bytes 28
  15.9 97.9 %all-to-all-start = ((f32[32,2,128,128]{3,2,1,0:T(8,128)}), f32[32,2,128,128]{3,2,1,0:T(8,128)}, u32[]{:S(2)}, u32[]{:S(2)}) async-start(f32[32,2,128,128]{3,2,1,0:T(8,128)} %bitcast.143), calls=%async_computation | async-start | bytes 8388608 | tf_op jit(solution)/shard_map/all_to_all | solution.py:232
  23.4 181.9 %all-reduce.6.cloned.1.call-start = ((), (), s32[]{:S(2)}) async-start(), calls=%async_computation.1 | async-start | bytes 3145728 | tf_op jit(solution)/shard_map/psum | solution.py:279
  126.1 4.7 collective-permute-start
  131.1 36.7 %collective-permute-start.1 = (f32[1536,256]{1,0:T(8,128)S(1)}, f32[1536,256]{1,0:T(8,128)}, u32[]{:S(2)}, u32[]{:S(2)}) collective-permute-start(f32[1536,256]{1,0:T(8,128)S(1)} %broadcast_select_fusion.6), channel_id=1, source_target_pairs={{0,8},{4,12},{8,0},{12,4},{1,9},{5,13},{9,1},{13,5},{2,10},{6,14},... | collective-permute-start | bytes 4718600 | tf_op jit(solution)/shard_map/ppermute | solution.py:31
  135.2 152.4 %all-reduce.8.cloned.1.call-start = ((), (), s32[]{:S(2)}) async-start(), calls=%async_computation.2 | async-start | bytes 3145728 | tf_op jit(solution)/shard_map/psum | solution.py:279
  205.3 4.7 copy-start.4
  216.4 3.8 collective-permute-start.2
  219.2 149.9 %all-reduce.10.cloned.1.call-start = ((), (), s32[]{:S(2)}) async-start(), calls=%async_computation.3 | async-start | bytes 3145728 | tf_op jit(solution)/shard_map/psum | solution.py:279
  221.7 36.5 %collective-permute-start.3 = (f32[1536,256]{1,0:T(8,128)S(1)}, f32[1536,256]{1,0:T(8,128)S(1)}, u32[]{:S(2)}, u32[]{:S(2)}) collective-permute-start(f32[1536,256]{1,0:T(8,128)S(1)} %broadcast_select_fusion.4), channel_id=1, source_target_pairs={{0,8},{4,12},{8,0},{12,4},{1,9},{5,13},{9,1},{13,5},{2,10},{6,14},... | collective-permute-start | bytes 4718600 | tf_op jit(solution)/shard_map/ppermute | solution.py:31
  235.5 3.7 copy-start.2
  287.7 4.7 copy-start.5
  298.7 3.8 collective-permute-start.4
  300.7 146.4 %all-reduce.12.cloned.1.call-start = ((), (), s32[]{:S(2)}) async-start(), calls=%async_computation.4 | async-start | bytes 3145728 | tf_op jit(solution)/shard_map/psum | solution.py:279
  304.1 36.5 %collective-permute-start.5 = (f32[1536,256]{1,0:T(8,128)S(1)}, f32[1536,256]{1,0:T(8,128)S(1)}, u32[]{:S(2)}, u32[]{:S(2)}) collective-permute-start(f32[1536,256]{1,0:T(8,128)S(1)} %broadcast_select_fusion.2), channel_id=1, source_target_pairs={{0,8},{4,12},{8,0},{12,4},{1,9},{5,13},{9,1},{13,5},{2,10},{6,14},... | collective-permute-start | bytes 4718600 | tf_op jit(solution)/shard_map/ppermute | solution.py:31
  317.7 3.7 copy-start.3
  378.5 1.1 copy-start.6
  378.5 3.6 collective-permute-start.6
  383.9 63.2 %collective-permute-start.7 = (f32[1536,256]{1,0:T(8,128)S(1)}, f32[1536,256]{1,0:T(8,128)}, u32[]{:S(2)}, u32[]{:S(2)}) collective-permute-start(f32[1536,256]{1,0:T(8,128)S(1)} %broadcast_select_fusion), channel_id=1, source_target_pairs={{0,8},{4,12},{8,0},{12,4},{1,9},{5,13},{9,1},{13,5},{2,10},{6,14},... | collective-permute-start | bytes 4718600 | tf_op jit(solution)/shard_map/ppermute | solution.py:31
  463.2 2.9 copy-start.1
Sparse Core Ops, SparseCore 0:
  135.4 69.8 all-reduce.5
  219.3 68.3 all-reduce.7
  300.8 68.3 all-reduce.9
  378.8 68.2 all-reduce.11
